TPU v7x, 256 devices: a whole 4x4x8 slice. The times are simulated.
256 devices in a mesh: row: 16 (over z_lo, y), col: 8 (over x, core), layer: 2 (over z_hi).
Axes of the slice: x: 4, y: 4, z: 8 (z_hi: 2, z_lo: 4; z = z_hi * 4 + z_lo), core: 2. Of those that a mesh axis runs over, the one named last changes fastest.
Arguments:
- density: float32 [2, 8192, 2048], P('layer', 'row', 'col'), may hold values from -6 to 6
- dens_mask: int32 [2, 128, 32], P('layer', 'row', 'col'), may hold values from 0 to 1, as said below
- hamiltonian: float32 [2, 2048, 16384], P('layer', 'row', 'col'), may hold values from -0.375 to 0.375
- ham_mask: int32 [2, 32, 256], P('layer', None, 'col'), may hold values from 0 to 1, as said below
- filter_mask: int32 [128, 256], P('row', 'col'), may hold values from 0 to 1, as said below
Outputs:
- product: float32 [8192, 16384], P('row', ('col', 'layer'))
Inputs may be any that keep to these rules, and one draw needn't show every extreme that they name: `dens_mask`: 1 where a density block is nonzero, else 0. `ham_mask`: 1 where a Hamiltonian block is nonzero, else 0. `filter_mask`: 1 where a result block is kept, else 0.
All inputs are finite; a program needn't handle non-finite values.
Results may differ from a plain program's by a relative error of at most 0.0001.
Values sent between devices are 32-bit elements; how exact they have to be, the bound alone decides.
No kernel may reach another device: no remote copies, remote signals or barrier semaphores. Data moves between devices by JAX's collectives and lax.ppermute only.
A program may use at most 128 MiB of HBM per device.

v0:
```python
import jax
import jax.numpy as jnp
from jax import lax
from jax.sharding import PartitionSpec as P

BLOCK = 64


def expand(block_mask):
    widened = jnp.repeat(block_mask.astype(jnp.float32), BLOCK, axis=-2)
    return jnp.repeat(widened, BLOCK, axis=-1)


def shards(density, dens_mask, hamiltonian, ham_mask, filter_mask):
    dens_vals = density * expand(dens_mask)
    ham_count = hamiltonian.shape[1]
    row_ids = lax.axis_index("row") * ham_count + jnp.arange(ham_count, dtype=jnp.int32)
    block_ids = row_ids // BLOCK
    one_hot = (
        block_ids[:, None] == jnp.arange(ham_mask.shape[1], dtype=jnp.int32)[None, :]
    ).astype(jnp.float32)
    picked = jnp.dot(
        one_hot,
        ham_mask[0].astype(jnp.float32),
        precision=lax.Precision.HIGHEST,
        preferred_element_type=jnp.float32,
    )
    ham_vals = hamiltonian * jnp.repeat(picked, BLOCK, axis=1)[None]
    kept = expand(filter_mask)
    ham_group = lax.all_gather(ham_vals, "row", axis=1, tiled=True)
    ham_part = ham_group[0]
    partial_value = jnp.dot(
        lax.all_gather(dens_vals, "col", axis=2, tiled=True)[0],
        ham_part,
        precision=lax.Precision.HIGHEST,
        preferred_element_type=jnp.float32,
    )
    return lax.psum_scatter(partial_value * kept, "layer", scatter_dimension=1, tiled=True)


def solution(mesh):
    return jax.shard_map(
        shards,
        mesh=mesh,
        in_specs=(
            P("layer", "row", "col"),
            P("layer", "row", "col"),
            P("layer", "row", "col"),
            P("layer", None, "col"),
            P("row", "col"),
        ),
        out_specs=P("row", ("col", "layer")),
        check_vma=False,
    )
```

profile of v0, /device:TPU:24, one launch (start us, length us, event | category | flops | bytes accessed | tf_op | source)
XLA Modules:
  0.0 425.3 jit_solution(16033029685912236478)
XLA Ops:
  6.5 0.0 copy-start.1
  6.5 0.0 copy-start
  6.5 0.0 all-gather.3.cloned.1.call-start
  6.5 1.3 copy.8
  7.8 0.7 convert_bitcast_fusion
  8.5 0.1 broadcast_in_dim.21
  8.6 0.1 broadcast_in_dim.22
  8.7 0.9 bitcast_multiply_fusion.1
  9.5 0.0 all-gather.3.cloned.1.call-update
  9.6 0.0 all-gather.5.cloned.1.call-start
  9.6 1.6 copy.9
  11.2 0.0 copy-done.1
  11.2 0.2 fusion.8
  11.4 1.1 bitcast_multiply_fusion
  12.5 0.0 all-gather.5.cloned.1.call-update
  12.5 0.0 reduce-scatter.2.cloned.1.call-start
  12.6 0.0 copy-done
  12.6 0.1 copy.10
  12.7 0.1 broadcast_in_dim.26
  12.8 0.1 reshape.35
  12.9 2.5 broadcast_in_dim.27
  15.4 5.5 %copy.11 = f32[512,2048]{1,0:T(8,128)} copy(f32[512,2048]{0,1:T(8,128)} %bitcast.24) | data formatting | bytes 8388608 | tf_op jit(solution)/shard_map/reshape | solution.py:11
  20.8 26.2 %all-gather.3.cloned.1.call-done = f32[1,512,2048]{1,2,0:T(8,128)} async-done(((f32[1,512,256]{1,2,0:T(8,128)}), f32[1,512,2048]{1,2,0:T(8,128)}) %all-gather.3.cloned.1.call-update) | async-done | bytes 4194320 | tf_op jit(solution)/shard_map/all_gather | solution.py:33
  47.0 203.9 %all-gather.5.cloned.1.call-done = f32[1,2048,2048]{1,2,0:T(8,128)} async-done(((f32[1,128,2048]{1,2,0:T(8,128)}), f32[1,2048,2048]{1,2,0:T(8,128)}) %all-gather.5.cloned.1.call-update) | async-done | bytes 16777232 | tf_op jit(solution)/shard_map/all_gather | solution.py:30
  250.9 57.7 %fusion.3 = f32[512,2048]{1,0:T(8,128)} fusion(f32[512,2048]{1,0:T(8,128)} %copy.11, f32[1,2048,2048]{1,2,0:T(8,128)} %all-gather.5.cloned.1.call-done, f32[1,512,2048]{1,2,0:T(8,128)} %all-gather.3.cloned.1.call-done), kind=kOutput, calls=%fused_computation.3 | convolution fusion | flops 25770852352 | bytes 29360128 | tf_op jit(solution)/shard_map/dot_general | solution.py:32
  308.6 0.0 reduce-scatter.2.cloned.1.call-update
  308.6 110.2 %reduce-scatter.2.cloned.1.call-done = f32[512,1024]{1,0:T(8,128)} async-done(((f32[512,2048]{1,0:T(8,128)}), f32[512,1024]{1,0:T(8,128)}) %reduce-scatter.2.cloned.1.call-update) | async-done | bytes 2097168 | tf_op jit(solution)/shard_map/reduce_scatter | solution.py:38
  (2 shorter events, 0.0 us)
Async XLA Ops:
  6.5 4.7 %copy-start.1 = (s32[1,32,32]{2,1,0:T(8,128)S(1)}, s32[1,32,32]{2,1,0:T(8,128)}, u32[]{:S(2)}) copy-start(s32[1,32,32]{2,1,0:T(8,128)} %param.8) | copy-start | bytes 12292
  6.5 6.1 %copy-start = (s32[8,32]{1,0:T(8,128)S(1)}, s32[8,32]{1,0:T(8,128)}, u32[]{:S(2)}) copy-start(s32[8,32]{1,0:T(8,128)} %param.9) | copy-start | bytes 3076
  6.5 40.5 %all-gather.3.cloned.1.call-start = ((), (), s32[]{:S(2)}) async-start(), calls=%async_computation.1 | async-start | bytes 4718592 | tf_op jit(solution)/shard_map/all_gather | solution.py:33
  9.6 241.4 %all-gather.5.cloned.1.call-start = ((), (), s32[]{:S(2)}) async-start(), calls=%async_computation.2 | async-start | bytes 17825792 | tf_op jit(solution)/shard_map/all_gather | solution.py:30
  12.5 406.3 %reduce-scatter.2.cloned.1.call-start = ((), (), s32[]{:S(2)}) async-start(), calls=%async_computation.3 | async-start | bytes 6291456 | tf_op jit(solution)/shard_map/reduce_scatter | solution.py:38
Sparse Core Ops, SparseCore 0:
  9.7 37.2 all-gather.2
  48.7 202.1 all-gather.4
  308.7 110.0 reduce-scatter.1
where the time goes:
time: 426 us; the launch traced here: 425 us
  waiting for transfers between devices  340 us (80%)
  matrix products  57.9 us (14%)
  between operations  13.2 us (3%)
  local copies, waits for them, and re-layouts  11.2 us (3%)
    all_gather x1, waiting for transfers between devices, shards(): ham_group = lax.all_gather(ham_vals, 'row', axis=1, tiled=True)  204 us
    reduce_scatter x1, waiting for transfers between devices, shards(): lax.psum_scatter(partial_value * kept, 'layer', scatter_dimension=1, tile...  110 us
    dot_general x1, matrix products, shards(): jnp.dot(lax.all_gather(dens_vals, 'col', axis=2, tiled=True)[0], ham_part...  57.7 us
    all_gather x1, waiting for transfers between devices, shards(): lax.all_gather(dens_vals, 'col', axis=2, tiled=True)[0]  26.2 us
  transfers between devices with their start and end apart: 3, of which 3 were waited for; matrix products, arithmetic and copies ran while one was open for 3% of the time, Pallas kernels for 0%

commit v1 on v0

v1 whole, which is shorter than its diff:
```python
import jax
import jax.numpy as jnp
from jax import lax
from jax.sharding import PartitionSpec as P

BLOCK = 64
N_CHUNKS = 2


def expand(block_mask):
    widened = jnp.repeat(block_mask.astype(jnp.float32), BLOCK, axis=-2)
    return jnp.repeat(widened, BLOCK, axis=-1)


def shards(density, dens_mask, hamiltonian, ham_mask, filter_mask):
    layer = lax.axis_index("layer")
    n_layer = lax.axis_size("layer")
    dens_vals = (density * expand(dens_mask))[0]
    ham_count = hamiltonian.shape[1]
    picked = lax.dynamic_slice_in_dim(
        ham_mask[0], lax.axis_index("row") * (ham_count // BLOCK), ham_count // BLOCK, axis=0
    )
    ham_vals = hamiltonian[0] * expand(picked)
    cols = ham_vals.shape[1]
    half = cols // n_layer
    width = half // N_CHUNKS
    kept = lax.dynamic_slice_in_dim(expand(filter_mask), layer * half, half, axis=1)

    dens_row = lax.all_gather(dens_vals, "col", axis=1, tiled=True)
    send_half = lax.dynamic_slice_in_dim(ham_vals, (1 - layer) * half, half, axis=1)
    keep_half = lax.dynamic_slice_in_dim(ham_vals, layer * half, half, axis=1)

    def panel(ham_half, j):
        ham_panel = lax.all_gather(ham_half[:, j * width:(j + 1) * width], "row", axis=0, tiled=True)
        return jnp.dot(
            dens_row,
            ham_panel,
            precision=lax.Precision.HIGHEST,
            preferred_element_type=jnp.float32,
        )

    perm = [(0, 1), (1, 0)]
    received = [lax.ppermute(panel(send_half, j), "layer", perm) for j in range(N_CHUNKS)]
    own = [panel(keep_half, j) for j in range(N_CHUNKS)]
    total = jnp.concatenate([a + b for a, b in zip(own, received)], axis=1)
    return total * kept


def solution(mesh):
    return jax.shard_map(
        shards,
        mesh=mesh,
        in_specs=(
            P("layer", "row", "col"),
            P("layer", "row", "col"),
            P("layer", "row", "col"),
            P("layer", None, "col"),
            P("row", "col"),
        ),
        out_specs=P("row", ("col", "layer")),
        check_vma=False,
    )
```

time: 426 us -> 481 us (1.13)
  waiting for transfers between devices: 340 us -> 408 us
  matrix products: 57.9 us -> 38.4 us
  starting transfers between devices: 0.09 us -> 10 us
    all_gather x2 -> x5, waiting for transfers between devices: 230 us -> 406 us  [the longest x4 374 us: panel(): lax.all_gather(ham_half[:, j * width:(j + 1) * width], 'row', axis=0, til...]
    reduce_scatter x1 -> x0, waiting for transfers between devices: 110 us -> none  [shards(): lax.psum_scatter(partial_value * kept, 'layer', scatter_dimension=1, tile...]
    dot_general x2 -> x4, matrix products: 57.9 us -> 38.4 us  [panel(): jnp.dot(dens_row, ham_panel, precision=lax.Precision.HIGHEST, preferred_e...]
    ppermute x0 -> x2, starting transfers between devices: none -> 9.84 us  [shards(): lax.ppermute(panel(send_half, j), 'layer', perm)]
    reshape x1 -> x0, local copies, waits for them, and re-layouts: 5.46 us -> none  [expand(): return jnp.repeat(widened, BLOCK, axis=-1)]
  transfers between devices with their start and end apart: 3 -> 7, of which waited for: 3 -> 5; matrix products, arithmetic and copies ran while one was open for 3% -> 7% of each run, Pallas kernels for 0% -> 0%
where the time goes in v1:
time: 481 us; the launch traced here: 479 us
  waiting for transfers between devices  408 us (85%)
  matrix products  38.4 us (8%)
  between operations  13.2 us (3%)
  starting transfers between devices  10 us (2%)
  local copies, waits for them, and re-layouts  6.81 us (1%)
    all_gather x4, waiting for transfers between devices, panel(): lax.all_gather(ham_half[:, j * width:(j + 1) * width], 'row', axis=0, til...  374 us
    dot_general x4, matrix products, panel(): jnp.dot(dens_row, ham_panel, precision=lax.Precision.HIGHEST, preferred_e...  38.4 us
    all_gather x1, waiting for transfers between devices, shards(): dens_row = lax.all_gather(dens_vals, 'col', axis=1, tiled=True)  31.8 us
    ppermute x2, starting transfers between devices, shards(): lax.ppermute(panel(send_half, j), 'layer', perm)  9.84 us
  transfers between devices with their start and end apart: 7, of which 5 were waited for; matrix products, arithmetic and copies ran while one was open for 7% of the time, Pallas kernels for 0%

profile of v1, /device:TPU:24, one launch (start us, length us, event | category | flops | bytes accessed | tf_op | source)
XLA Modules:
  0.0 479.2 jit_solution(12785967201112321304)
XLA Ops:
  6.5 0.0 all-gather.15.cloned.1.call-start
  6.5 1.2 copy.11
  7.8 0.7 convert_bitcast_fusion
  8.5 0.1 broadcast_in_dim.22
  8.5 0.1 broadcast_in_dim.23
  8.6 0.9 bitcast_multiply_fusion.1
  9.5 0.0 all-gather.15.cloned.1.call-update
  9.5 0.0 all-gather.9.cloned.1.call-start
  9.6 0.7 fusion.15
  10.3 0.1 copy.13
  10.4 0.1 broadcast_in_dim.26
  10.4 0.1 reshape.23
  10.5 1.6 copy.12
  12.1 0.1 bitcast_multiply_fusion
  12.2 1.0 constant_dynamic-slice_fusion.1
  13.2 0.0 all-gather.9.cloned.1.call-update
  13.2 0.0 all-gather.13.cloned.1.call-start
  13.3 0.7 all-gather.13.cloned.1.call-update
  13.9 0.0 all-gather.7.cloned.1.call-start
  14.0 0.5 all-gather.7.cloned.1.call-update
  14.5 0.0 all-gather.11.cloned.1.call-start
  14.6 0.5 all-gather.11.cloned.1.call-update
  15.1 31.8 %all-gather.15.cloned.1.call-done = f32[1,512,2048]{1,2,0:T(8,128)} async-done(((f32[1,512,256]{1,2,0:T(8,128)}), f32[1,512,2048]{1,2,0:T(8,128)}) %all-gather.15.cloned.1.call-update) | async-done | bytes 4194320 | tf_op jit(solution)/shard_map/all_gather | solution.py:29
  46.9 91.4 %all-gather.9.cloned.1.call-done = f32[2048,512]{0,1:T(8,128)} async-done(((f32[128,512]{0,1:T(8,128)}), f32[2048,512]{0,1:T(8,128)}) %all-gather.9.cloned.1.call-update) | async-done | bytes 4194320 | tf_op jit(solution)/shard_map/all_gather | solution.py:34
  138.4 9.3 %fusion.4 = f32[512,512]{0,1:T(8,128)S(1)} fusion(f32[2048,512]{0,1:T(8,128)} %all-gather.9.cloned.1.call-done, f32[1,512,2048]{1,2,0:T(8,128)} %all-gather.15.cloned.1.call-done), kind=kOutput, calls=%fused_computation.4 | convolution fusion | flops 6442450944 | bytes 9437184 | tf_op jit(solution)/shard_map/dot_general | solution.py:35
  147.6 0.0 copy-start
  147.7 3.6 collective-permute-start
  151.3 101.4 %all-gather.13.cloned.1.call-done = f32[2048,512]{0,1:T(8,128)} async-done(((f32[128,512]{0,1:T(8,128)}), f32[2048,512]{0,1:T(8,128)}) %all-gather.13.cloned.1.call-update) | async-done | bytes 4194320 | tf_op jit(solution)/shard_map/all_gather | solution.py:34
  252.6 10.2 %fusion = f32[512,512]{0,1:T(8,128)} fusion(f32[2048,512]{0,1:T(8,128)} %all-gather.13.cloned.1.call-done, f32[1,512,2048]{1,2,0:T(8,128)} %all-gather.15.cloned.1.call-done), kind=kOutput, calls=%fused_computation | convolution fusion | flops 6442450944 | bytes 9437184 | tf_op jit(solution)/shard_map/dot_general | solution.py:35
  262.9 6.2 %collective-permute-start.1 = (f32[512,512]{0,1:T(8,128)}, f32[512,512]{0,1:T(8,128)S(1)}, u32[]{:S(2)}, u32[]{:S(2)}) collective-permute-start(f32[512,512]{0,1:T(8,128)} %fusion), channel_id=1, source_target_pairs={{0,1},{1,0},{2,3},{3,2},{4,5},{5,4},{6,7},{7,6},{8,9},{9,8},{10,11... | collective-permute-start | bytes 3145736 | tf_op jit(solution)/shard_map/ppermute | solution.py:43
  269.1 0.0 copy-done
  269.1 0.1 copy.16
  269.2 0.1 broadcast_in_dim.28
  269.3 0.1 reshape.25
  269.4 102.1 %all-gather.7.cloned.1.call-done = f32[2048,512]{0,1:T(8,128)} async-done(((f32[128,512]{0,1:T(8,128)}), f32[2048,512]{0,1:T(8,128)}) %all-gather.7.cloned.1.call-update) | async-done | bytes 4194320 | tf_op jit(solution)/shard_map/all_gather | solution.py:34
  371.4 0.0 collective-permute-done
  371.4 9.4 %fusion.8 = f32[512,512]{0,1:T(8,128)S(1)} fusion(f32[512,512]{0,1:T(8,128)S(1)} %collective-permute-done, f32[2048,512]{0,1:T(8,128)} %all-gather.7.cloned.1.call-done, f32[1,512,2048]{1,2,0:T(8,128)} %all-gather.15.cloned.1.call-done), kind=kOutput, calls=%fused_computation.9 | convolution fusion | flops 6442713088 | bytes 10485760 | tf_op jit(solution)/shard_map/dot_general | solution.py:35
  380.9 79.5 %all-gather.11.cloned.1.call-done = f32[2048,512]{0,1:T(8,128)} async-done(((f32[128,512]{0,1:T(8,128)}), f32[2048,512]{0,1:T(8,128)}) %all-gather.11.cloned.1.call-update) | async-done | bytes 4194320 | tf_op jit(solution)/shard_map/all_gather | solution.py:34
  460.4 0.0 collective-permute-done.1
  460.4 9.5 %fusion.11 = f32[512,512]{0,1:T(8,128)S(1)} fusion(f32[512,512]{0,1:T(8,128)S(1)} %collective-permute-done.1, f32[2048,512]{0,1:T(8,128)} %all-gather.11.cloned.1.call-done, f32[1,512,2048]{1,2,0:T(8,128)} %all-gather.15.cloned.1.call-done), kind=kOutput, calls=%fused_computation.10 | convolution fusion | flops 6442713088 | bytes 10485760 | tf_op jit(solution)/shard_map/dot_general | solution.py:35
  469.8 0.5 broadcast_in_dim.29
  470.4 0.5 maximum_multiply_fusion
  470.9 1.8 copy.17
  (1 shorter events, 0.0 us)
Async XLA Ops:
  6.5 40.4 %all-gather.15.cloned.1.call-start = ((), (), s32[]{:S(2)}) async-start(), calls=%async_computation.4 | async-start | bytes 4718592 | tf_op jit(solution)/shard_map/all_gather | solution.py:29
  9.5 128.8 %all-gather.9.cloned.1.call-start = ((), (), s32[]{:S(2)}) async-start(), calls=%async_computation.1 | async-start | bytes 4456448 | tf_op jit(solution)/shard_map/all_gather | solution.py:34
  13.2 239.4 %all-gather.13.cloned.1.call-start = ((), (), s32[]{:S(2)}) async-start(), calls=%async_computation.3 | async-start | bytes 4456448 | tf_op jit(solution)/shard_map/all_gather | solution.py:34
  13.9 357.5 %all-gather.7.cloned.1.call-start = ((), (), s32[]{:S(2)}) async-start(), calls=%async_computation | async-start | bytes 4456448 | tf_op jit(solution)/shard_map/all_gather | solution.py:34
  14.5 445.8 %all-gather.11.cloned.1.call-start = ((), (), s32[]{:S(2)}) async-start(), calls=%async_computation.2 | async-start | bytes 4456448 | tf_op jit(solution)/shard_map/all_gather | solution.py:34
  147.6 121.5 %copy-start = (s32[8,32]{1,0:T(8,128)S(1)}, s32[8,32]{1,0:T(8,128)}, u32[]{:S(2)}) copy-start(s32[8,32]{1,0:T(8,128)} %param.9) | copy-start | bytes 3076
  147.7 223.8 %collective-permute-start = (f32[512,512]{0,1:T(8,128)S(1)}, f32[512,512]{0,1:T(8,128)S(1)}, u32[]{:S(2)}, u32[]{:S(2)}) collective-permute-start(f32[512,512]{0,1:T(8,128)S(1)} %fusion.4), channel_id=1, source_target_pairs={{0,1},{1,0},{2,3},{3,2},{4,5},{5,4},{6,7},{7,6},{8,9},{9,8},{10,11... | collective-permute-start | bytes 3145736 | tf_op jit(solution)/shard_map/ppermute | solution.py:43
  262.9 197.5 %collective-permute-start.1 = (f32[512,512]{0,1:T(8,128)}, f32[512,512]{0,1:T(8,128)S(1)}, u32[]{:S(2)}, u32[]{:S(2)}) collective-permute-start(f32[512,512]{0,1:T(8,128)} %fusion), channel_id=1, source_target_pairs={{0,1},{1,0},{2,3},{3,2},{4,5},{5,4},{6,7},{7,6},{8,9},{9,8},{10,11... | collective-permute-start | bytes 3145736 | tf_op jit(solution)/shard_map/ppermute | solution.py:43
Sparse Core Ops, SparseCore 0:
  9.6 37.2 all-gather.14
  48.6 89.6 all-gather.8
  140.1 112.5 all-gather.12
  254.2 117.1 all-gather.6
  373.0 87.3 all-gather.10

commit v2 on v1

v2 whole, which is shorter than its diff:
```python
import jax
import jax.numpy as jnp
from jax import lax
from jax.sharding import PartitionSpec as P

BLOCK = 64


def expand(block_mask):
    widened = jnp.repeat(block_mask.astype(jnp.float32), BLOCK, axis=-2)
    return jnp.repeat(widened, BLOCK, axis=-1)


def gather_cols(block, axis_name, n):
    parts = [block]
    for shift in range(1, n):
        parts.append(lax.ppermute(block, axis_name, [((i + shift) % n, i) for i in range(n)]))
    twice = jnp.concatenate(parts + parts, axis=1)
    start = (n - lax.axis_index(axis_name)) * block.shape[1]
    return lax.dynamic_slice_in_dim(twice, start, n * block.shape[1], axis=1)


def product_dot(a, b):
    return jnp.dot(a, b, precision=lax.Precision.HIGHEST, preferred_element_type=jnp.float32)


def shards(density, dens_mask, hamiltonian, ham_mask, filter_mask, n_col):
    layer = lax.axis_index("layer")
    dens_vals = (density * expand(dens_mask))[0]
    ham_count = hamiltonian.shape[1]
    picked = lax.dynamic_slice_in_dim(
        ham_mask[0], lax.axis_index("row") * (ham_count // BLOCK), ham_count // BLOCK, axis=0
    )
    ham_vals = hamiltonian[0] * expand(picked)
    half = ham_vals.shape[1] // 2
    kept = lax.dynamic_slice_in_dim(expand(filter_mask), layer * half, half, axis=1)

    send_half = lax.dynamic_slice_in_dim(ham_vals, (1 - layer) * half, half, axis=1)
    keep_half = lax.dynamic_slice_in_dim(ham_vals, layer * half, half, axis=1)
    ham_send = lax.all_gather(send_half, "row", axis=0, tiled=True)
    dens_row = gather_cols(dens_vals, "col", n_col)
    received = lax.ppermute(product_dot(dens_row, ham_send), "layer", [(0, 1), (1, 0)])
    ham_keep = lax.all_gather(keep_half, "row", axis=0, tiled=True)
    own = product_dot(dens_row, ham_keep)
    return (own + received) * kept


def solution(mesh):
    n_col = mesh.shape["col"]
    return jax.shard_map(
        lambda *args: shards(*args, n_col),
        mesh=mesh,
        in_specs=(
            P("layer", "row", "col"),
            P("layer", "row", "col"),
            P("layer", "row", "col"),
            P("layer", None, "col"),
            P("row", "col"),
        ),
        out_specs=P("row", ("col", "layer")),
        check_vma=False,
    )
```

time: 481 us -> 386 us (0.80)
  the two profiles are of different devices: /device:TPU:24 before, /device:TPU:78 now
where the time goes in v2:
time: 386 us; the launch traced here: 385 us
  waiting for transfers between devices  274 us (71%)
  matrix products  62.6 us (16%)
  local copies, waits for them, and re-layouts  19.7 us (5%)
  between operations  13.5 us (3%)
  starting transfers between devices  13.4 us (3%)
    all_gather x1, waiting for transfers between devices, shards(): ham_keep = lax.all_gather(keep_half, 'row', axis=0, tiled=True)  175 us
    dot_general x2, matrix products, product_dot(): jnp.dot(a, b, precision=lax.Precision.HIGHEST, preferred_element_type=jnp...  62.6 us
    all_gather x1, waiting for transfers between devices, shards(): ham_send = lax.all_gather(send_half, 'row', axis=0, tiled=True)  55.2 us
    ppermute x7, waiting for transfers between devices, gather_cols(): lax.ppermute(block, axis_name, [((i + shift) % n, i) for i in range(n)])  44 us
    unnamed x21, local copies, waits for them, and re-layouts  16.4 us
    ppermute x7, starting transfers between devices, gather_cols(): lax.ppermute(block, axis_name, [((i + shift) % n, i) for i in range(n)])  8.62 us
  transfers between devices with their start and end apart: 10, of which 5 were waited for; matrix products, arithmetic and copies ran while one was open for 13% of the time, Pallas kernels for 0%

profile of v2, /device:TPU:78, one launch (start us, length us, event | category | flops | bytes accessed | tf_op | source)
XLA Modules:
  0.0 385.5 jit_solution(14352574710294579853)
XLA Ops:
  6.5 0.7 fusion.9
  7.2 0.1 copy.9
  7.3 0.1 broadcast_in_dim.26
  7.4 0.1 reshape.23
  7.5 1.6 copy.8
  9.1 0.1 bitcast_multiply_fusion
  9.2 1.0 constant_dynamic-slice_fusion.2
  10.2 0.0 all-gather.3.cloned.1.call-start
  10.3 0.7 all-gather.3.cloned.1.call-update
  11.0 1.2 copy.7
  12.3 0.1 broadcast_in_dim.22
  12.3 0.1 broadcast_in_dim.23
  12.4 0.9 constant_dynamic-update-slice_fusion.15
  13.3 0.3 collective-permute-start
  13.6 0.6 collective-permute-start.1
  14.2 0.9 collective-permute-start.2
  15.1 2.4 collective-permute-start.3
  17.5 2.0 collective-permute-start.4
  19.5 6.3 %collective-permute-done = f32[512,256]{0,1:T(8,128)S(1)} collective-permute-done((f32[512,256]{0,1:T(8,128)S(1)}, f32[512,256]{0,1:T(8,128)S(1)}, u32[]{:S(2)}, u32[]{:S(2)}) %collective-permute-start) | collective-permute-done | bytes 524320 | tf_op jit(solution)/shard_map/ppermute | solution.py:17
  25.8 2.4 collective-permute-start.5
  28.2 0.8 constant_dynamic-update-slice_fusion.14
  29.1 33.3 %collective-permute-done.1 = f32[512,256]{0,1:T(8,128)S(1)} collective-permute-done((f32[512,256]{0,1:T(8,128)S(1)}, f32[512,256]{0,1:T(8,128)S(1)}, u32[]{:S(2)}, u32[]{:S(2)}) %collective-permute-start.1) | collective-permute-done | bytes 524320 | tf_op jit(solution)/shard_map/ppermute | solution.py:17
  62.4 0.9 constant_dynamic-update-slice_fusion.13
  63.3 0.8 constant_dynamic-update-slice_fusion.12
  64.1 0.9 constant_dynamic-update-slice_fusion.11
  65.0 0.8 constant_dynamic-update-slice_fusion.10
  65.8 0.8 constant_dynamic-update-slice_fusion.9
  66.6 4.4 %collective-permute-done.6 = f32[512,256]{0,1:T(8,128)S(1)} collective-permute-done((f32[512,256]{0,1:T(8,128)S(1)}, f32[512,256]{0,1:T(8,128)S(1)}, u32[]{:S(2)}, u32[]{:S(2)}) %collective-permute-start.6) | collective-permute-done | bytes 524320 | tf_op jit(solution)/shard_map/ppermute | solution.py:17
  71.0 0.8 constant_dynamic-update-slice_fusion.8
  71.8 0.8 constant_dynamic-update-slice_fusion.7
  72.7 0.8 constant_dynamic-update-slice_fusion.6
  73.5 0.9 constant_dynamic-update-slice_fusion.5
  74.4 0.8 constant_dynamic-update-slice_fusion.4
  75.2 0.8 constant_dynamic-update-slice_fusion.3
  76.1 0.8 constant_dynamic-update-slice_fusion.2
  76.9 0.8 constant_dynamic-update-slice_fusion.1
  77.7 0.9 constant_dynamic-update-slice_fusion
  78.6 55.2 %all-gather.5.cloned.1.call-done = f32[2048,1024]{0,1:T(8,128)} async-done(((f32[128,1024]{0,1:T(8,128)}), f32[2048,1024]{0,1:T(8,128)}) %all-gather.5.cloned.1.call-update) | async-done | bytes 8388624 | tf_op jit(solution)/shard_map/all_gather | solution.py:40
  133.8 30.9 %fusion = f32[512,1024]{1,0:T(8,128)} fusion(f32[2048,1024]{0,1:T(8,128)} %all-gather.5.cloned.1.call-done, f32[512,4096]{0,1:T(8,128)} %constant_dynamic-update-slice_fusion, s32[]{:T(128)S(6)} %select_n.13), kind=kOutput, calls=%fused_computation | convolution fusion | flops 12884901888 | bytes 14680068 | tf_op jit(solution)/shard_map/dot_general | solution.py:24
  164.7 4.8 %collective-permute-start.7 = (f32[512,1024]{1,0:T(8,128)}, f32[512,1024]{1,0:T(8,128)}, u32[]{:S(2)}, u32[]{:S(2)}) collective-permute-start(f32[512,1024]{1,0:T(8,128)} %fusion), channel_id=1, source_target_pairs={{0,1},{1,0},{2,3},{3,2},{4,5},{5,4},{6,7},{7,6},{8,9},{9,8},{10,11... | collective-permute-start | bytes 6291464 | tf_op jit(solution)/shard_map/ppermute | solution.py:42
  169.5 0.1 copy.10
  169.6 0.1 broadcast_in_dim.28
  169.7 0.1 reshape.25
  169.8 0.5 broadcast_in_dim.29
  170.3 0.2 constant_dynamic-slice_fusion
  170.5 1.8 copy.12
  172.3 174.6 %all-gather.3.cloned.1.call-done = f32[2048,1024]{0,1:T(8,128)} async-done(((f32[128,1024]{0,1:T(8,128)}), f32[2048,1024]{0,1:T(8,128)}) %all-gather.3.cloned.1.call-update) | async-done | bytes 8388624 | tf_op jit(solution)/shard_map/all_gather | solution.py:43
  346.9 31.7 %add_multiply_fusion = f32[512,1024]{1,0:T(8,128)} fusion(f32[512,1024]{1,0:T(8,128)} %copy.12, f32[512,1024]{1,0:T(8,128)} %collective-permute-done.7, f32[2048,1024]{0,1:T(8,128)} %all-gather.3.cloned.1.call-done, f32[512,4096]{0,1:T(8,128)} %constant_dynamic-update-slice_fusion, s32[]{:T(128)S(6)} %select_n.13), kind=kOutput, calls=%fused_computation.4 | convolution fusion | flops 12885950464 | bytes 18874372 | tf_op jit(solution)/shard_map/dot_general | solution.py:24
  (14 shorter events, 0.0 us)
Async XLA Ops:
  6.5 5.7 %copy-start.1 = (s32[1,8,4]{1,2,0:T(4,128)S(1)}, s32[1,8,4]{1,2,0:T(4,128)}, u32[]{:S(2)}) copy-start(s32[1,8,4]{1,2,0:T(4,128)} %param.6) | copy-start | bytes 388
  6.5 127.3 %all-gather.5.cloned.1.call-start = ((), (), s32[]{:S(2)}) async-start(), calls=%async_computation.1 | async-start | bytes 8912896 | tf_op jit(solution)/shard_map/all_gather | solution.py:40
  10.2 336.7 %all-gather.3.cloned.1.call-start = ((), (), s32[]{:S(2)}) async-start(), calls=%async_computation | async-start | bytes 8912896 | tf_op jit(solution)/shard_map/all_gather | solution.py:43
  13.3 12.5 %collective-permute-start = (f32[512,256]{0,1:T(8,128)S(1)}, f32[512,256]{0,1:T(8,128)S(1)}, u32[]{:S(2)}, u32[]{:S(2)}) collective-permute-start(f32[512,256]{0,1:T(8,128)S(1)} %bitcast.23), channel_id=1, source_target_pairs={{2,0},{4,2},{6,4},{8,6},{10,8},{12,10},{14,12},{0,14},{3,1},{5,3},... | collective-permute-start | bytes 1572872 | tf_op jit(solution)/shard_map/ppermute | solution.py:17
  13.6 48.8 %collective-permute-start.1 = (f32[512,256]{0,1:T(8,128)S(1)}, f32[512,256]{0,1:T(8,128)S(1)}, u32[]{:S(2)}, u32[]{:S(2)}) collective-permute-start(f32[512,256]{0,1:T(8,128)S(1)} %bitcast.24), channel_id=1, source_target_pairs={{4,0},{6,2},{8,4},{10,6},{12,8},{14,10},{0,12},{2,14},{5,1},{7,3},... | collective-permute-start | bytes 1572872 | tf_op jit(solution)/shard_map/ppermute | solution.py:17
  14.2 49.1 %collective-permute-start.2 = (f32[512,256]{0,1:T(8,128)S(1)}, f32[512,256]{0,1:T(8,128)S(1)}, u32[]{:S(2)}, u32[]{:S(2)}) collective-permute-start(f32[512,256]{0,1:T(8,128)S(1)} %bitcast.25), channel_id=1, source_target_pairs={{6,0},{8,2},{10,4},{12,6},{14,8},{0,10},{2,12},{4,14},{7,1},{9,3},... | collective-permute-start | bytes 1572872 | tf_op jit(solution)/shard_map/ppermute | solution.py:17
  15.1 49.0 %collective-permute-start.3 = (f32[512,256]{0,1:T(8,128)S(1)}, f32[512,256]{0,1:T(8,128)S(1)}, u32[]{:S(2)}, u32[]{:S(2)}) collective-permute-start(f32[512,256]{0,1:T(8,128)S(1)} %bitcast.26), channel_id=1, source_target_pairs={{8,0},{10,2},{12,4},{14,6},{0,8},{2,10},{4,12},{6,14},{9,1},{11,3}... | collective-permute-start | bytes 1572872 | tf_op jit(solution)/shard_map/ppermute | solution.py:17
  17.5 47.4 %collective-permute-start.4 = (f32[512,256]{0,1:T(8,128)S(1)}, f32[512,256]{0,1:T(8,128)S(1)}, u32[]{:S(2)}, u32[]{:S(2)}) collective-permute-start(f32[512,256]{0,1:T(8,128)S(1)} %bitcast.27), channel_id=1, source_target_pairs={{10,0},{12,2},{14,4},{0,6},{2,8},{4,10},{6,12},{8,14},{11,1},{13,3... | collective-permute-start | bytes 1572872 | tf_op jit(solution)/shard_map/ppermute | solution.py:17
  25.8 40.0 %collective-permute-start.5 = (f32[512,256]{0,1:T(8,128)S(1)}, f32[512,256]{0,1:T(8,128)S(1)}, u32[]{:S(2)}, u32[]{:S(2)}) collective-permute-start(f32[512,256]{0,1:T(8,128)S(1)} %bitcast.28), channel_id=1, source_target_pairs={{12,0},{14,2},{0,4},{2,6},{4,8},{6,10},{8,12},{10,14},{13,1},{15,3... | collective-permute-start | bytes 1572872 | tf_op jit(solution)/shard_map/ppermute | solution.py:17
  62.4 8.6 %collective-permute-start.6 = (f32[512,256]{0,1:T(8,128)S(1)}, f32[512,256]{0,1:T(8,128)S(1)}, u32[]{:S(2)}, u32[]{:S(2)}) collective-permute-start(f32[512,256]{0,1:T(8,128)S(1)} %bitcast.29), channel_id=1, source_target_pairs={{14,0},{0,2},{2,4},{4,6},{6,8},{8,10},{10,12},{12,14},{15,1},{1,3}... | collective-permute-start | bytes 1572872 | tf_op jit(solution)/shard_map/ppermute | solution.py:17
  76.9 92.6 %copy-start = (s32[8,32]{1,0:T(8,128)S(1)}, s32[8,32]{1,0:T(8,128)}, u32[]{:S(2)}) copy-start(s32[8,32]{1,0:T(8,128)} %param.9) | copy-start | bytes 3076
  164.7 182.2 %collective-permute-start.7 = (f32[512,1024]{1,0:T(8,128)}, f32[512,1024]{1,0:T(8,128)}, u32[]{:S(2)}, u32[]{:S(2)}) collective-permute-start(f32[512,1024]{1,0:T(8,128)} %fusion), channel_id=1, source_target_pairs={{0,1},{1,0},{2,3},{3,2},{4,5},{5,4},{6,7},{7,6},{8,9},{9,8},{10,11... | collective-permute-start | bytes 6291464 | tf_op jit(solution)/shard_map/ppermute | solution.py:42
Sparse Core Ops, SparseCore 0:
  10.4 123.4 all-gather.4
  135.5 211.3 all-gather.2

commit v3 on v2

--- a/solution.py
+++ b/solution.py
@@ -21,7 +21,7 @@
 
 
 def product_dot(a, b):
-    return jnp.dot(a, b, precision=lax.Precision.HIGHEST, preferred_element_type=jnp.float32)
+    return jnp.dot(a, b, precision=lax.Precision.HIGH, preferred_element_type=jnp.float32)
 
 
 def shards(density, dens_mask, hamiltonian, ham_mask, filter_mask, n_col):

time: 386 us -> 368 us (0.953)
  the two profiles are of different devices: /device:TPU:78 before, /device:TPU:64 now
where the time goes in v3:
time: 368 us; the launch traced here: 367 us
  waiting for transfers between devices  285 us (77%)
  matrix products  36.8 us (10%)
  local copies, waits for them, and re-layouts  19.7 us (5%)
  between operations  13.5 us (4%)
  starting transfers between devices  10.5 us (3%)
    all_gather x1, waiting for transfers between devices, shards(): ham_keep = lax.all_gather(keep_half, 'row', axis=0, tiled=True)  181 us
    all_gather x1, waiting for transfers between devices, shards(): ham_send = lax.all_gather(send_half, 'row', axis=0, tiled=True)  56.3 us
    ppermute x7, waiting for transfers between devices, gather_cols(): lax.ppermute(block, axis_name, [((i + shift) % n, i) for i in range(n)])  46.6 us
    dot_general x2, matrix products, product_dot(): jnp.dot(a, b, precision=lax.Precision.HIGH, preferred_element_type=jnp.fl...  36.8 us
    unnamed x21, local copies, waits for them, and re-layouts  16.4 us
  transfers between devices with their start and end apart: 10, of which 5 were waited for; matrix products, arithmetic and copies ran while one was open for 10% of the time, Pallas kernels for 0%

profile of v3, /device:TPU:64, one launch (start us, length us, event | category | flops | bytes accessed | tf_op | source)
XLA Modules:
  0.0 367.4 jit_solution(11268462630033968661)
XLA Ops:
  6.5 0.7 fusion.9
  7.2 0.1 copy.9
  7.3 0.1 broadcast_in_dim.26
  7.4 0.1 reshape.23
  7.5 1.6 copy.8
  9.1 0.1 bitcast_multiply_fusion
  9.2 1.0 constant_dynamic-slice_fusion.2
  10.2 0.0 all-gather.5.cloned.1.call-update
  10.2 0.0 all-gather.3.cloned.1.call-start
  10.3 0.7 all-gather.3.cloned.1.call-update
  11.0 1.2 copy.7
  12.3 0.1 broadcast_in_dim.22
  12.3 0.1 broadcast_in_dim.23
  12.4 0.9 constant_dynamic-update-slice_fusion.15
  13.3 2.2 collective-permute-start
  15.5 0.8 collective-permute-start.1
  16.4 0.4 collective-permute-start.2
  16.7 2.7 collective-permute-start.3
  19.5 8.3 %collective-permute-done = f32[512,256]{0,1:T(8,128)S(1)} collective-permute-done((f32[512,256]{0,1:T(8,128)S(1)}, f32[512,256]{0,1:T(8,128)S(1)}, u32[]{:S(2)}, u32[]{:S(2)}) %collective-permute-start) | collective-permute-done | bytes 524320 | tf_op jit(solution)/shard_map/ppermute | solution.py:17
  27.7 0.8 constant_dynamic-update-slice_fusion.14
  28.6 32.7 %collective-permute-done.1 = f32[512,256]{0,1:T(8,128)S(1)} collective-permute-done((f32[512,256]{0,1:T(8,128)S(1)}, f32[512,256]{0,1:T(8,128)S(1)}, u32[]{:S(2)}, u32[]{:S(2)}) %collective-permute-start.1) | collective-permute-done | bytes 524320 | tf_op jit(solution)/shard_map/ppermute | solution.py:17
  61.3 0.9 constant_dynamic-update-slice_fusion.13
  62.2 0.0 collective-permute-done.2
  62.2 0.8 constant_dynamic-update-slice_fusion.12
  63.0 0.9 constant_dynamic-update-slice_fusion.11
  63.9 0.8 constant_dynamic-update-slice_fusion.10
  64.7 0.8 constant_dynamic-update-slice_fusion.9
  65.6 5.6 %collective-permute-done.6 = f32[512,256]{0,1:T(8,128)S(1)} collective-permute-done((f32[512,256]{0,1:T(8,128)S(1)}, f32[512,256]{0,1:T(8,128)S(1)}, u32[]{:S(2)}, u32[]{:S(2)}) %collective-permute-start.6) | collective-permute-done | bytes 524320 | tf_op jit(solution)/shard_map/ppermute | solution.py:17
  71.1 0.8 constant_dynamic-update-slice_fusion.8
  72.0 0.8 constant_dynamic-update-slice_fusion.7
  72.8 0.8 constant_dynamic-update-slice_fusion.6
  73.6 0.9 constant_dynamic-update-slice_fusion.5
  74.5 0.8 constant_dynamic-update-slice_fusion.4
  75.4 0.8 constant_dynamic-update-slice_fusion.3
  76.2 0.8 constant_dynamic-update-slice_fusion.2
  77.0 0.8 constant_dynamic-update-slice_fusion.1
  77.9 0.9 constant_dynamic-update-slice_fusion
  78.7 56.3 %all-gather.5.cloned.1.call-done = f32[2048,1024]{0,1:T(8,128)} async-done(((f32[128,1024]{0,1:T(8,128)}), f32[2048,1024]{0,1:T(8,128)}) %all-gather.5.cloned.1.call-update) | async-done | bytes 8388624 | tf_op jit(solution)/shard_map/all_gather | solution.py:40
  135.1 18.0 %fusion = f32[512,1024]{1,0:T(8,128)} fusion(f32[2048,1024]{0,1:T(8,128)} %all-gather.5.cloned.1.call-done, f32[512,4096]{0,1:T(8,128)} %constant_dynamic-update-slice_fusion, s32[]{:T(128)S(6)} %select_n.13), kind=kOutput, calls=%fused_computation | convolution fusion | flops 6442450944 | bytes 14680068 | tf_op jit(solution)/shard_map/dot_general | solution.py:24
  153.0 4.4 %collective-permute-start.7 = (f32[512,1024]{1,0:T(8,128)}, f32[512,1024]{1,0:T(8,128)}, u32[]{:S(2)}, u32[]{:S(2)}) collective-permute-start(f32[512,1024]{1,0:T(8,128)} %fusion), channel_id=1, source_target_pairs={{0,1},{1,0},{2,3},{3,2},{4,5},{5,4},{6,7},{7,6},{8,9},{9,8},{10,11... | collective-permute-start | bytes 6291464 | tf_op jit(solution)/shard_map/ppermute | solution.py:42
  157.4 0.1 copy.10
  157.5 0.1 broadcast_in_dim.28
  157.6 0.1 reshape.25
  157.7 0.5 broadcast_in_dim.29
  158.2 0.2 constant_dynamic-slice_fusion
  158.4 1.8 copy.12
  160.2 181.5 %all-gather.3.cloned.1.call-done = f32[2048,1024]{0,1:T(8,128)} async-done(((f32[128,1024]{0,1:T(8,128)}), f32[2048,1024]{0,1:T(8,128)}) %all-gather.3.cloned.1.call-update) | async-done | bytes 8388624 | tf_op jit(solution)/shard_map/all_gather | solution.py:43
  341.7 18.8 %add_multiply_fusion = f32[512,1024]{1,0:T(8,128)} fusion(f32[512,1024]{1,0:T(8,128)} %copy.12, f32[512,1024]{1,0:T(8,128)} %collective-permute-done.7, f32[2048,1024]{0,1:T(8,128)} %all-gather.3.cloned.1.call-done, f32[512,4096]{0,1:T(8,128)} %constant_dynamic-update-slice_fusion, s32[]{:T(128)S(6)} %select_n.13), kind=kOutput, calls=%fused_computation.4 | convolution fusion | flops 6443499520 | bytes 18874372 | tf_op jit(solution)/shard_map/dot_general | solution.py:24
  (14 shorter events, 0.0 us)
Async XLA Ops:
  6.5 5.7 %copy-start.1 = (s32[1,8,4]{1,2,0:T(4,128)S(1)}, s32[1,8,4]{1,2,0:T(4,128)}, u32[]{:S(2)}) copy-start(s32[1,8,4]{1,2,0:T(4,128)} %param.6) | copy-start | bytes 388
  6.5 128.5 %all-gather.5.cloned.1.call-start = ((), (), s32[]{:S(2)}) async-start(), calls=%async_computation.1 | async-start | bytes 8912896 | tf_op jit(solution)/shard_map/all_gather | solution.py:40
  10.2 331.5 %all-gather.3.cloned.1.call-start = ((), (), s32[]{:S(2)}) async-start(), calls=%async_computation | async-start | bytes 8912896 | tf_op jit(solution)/shard_map/all_gather | solution.py:43
  13.3 14.4 %collective-permute-start = (f32[512,256]{0,1:T(8,128)S(1)}, f32[512,256]{0,1:T(8,128)S(1)}, u32[]{:S(2)}, u32[]{:S(2)}) collective-permute-start(f32[512,256]{0,1:T(8,128)S(1)} %bitcast.23), channel_id=1, source_target_pairs={{2,0},{4,2},{6,4},{8,6},{10,8},{12,10},{14,12},{0,14},{3,1},{5,3},... | collective-permute-start | bytes 1572872 | tf_op jit(solution)/shard_map/ppermute | solution.py:17
  15.5 45.8 %collective-permute-start.1 = (f32[512,256]{0,1:T(8,128)S(1)}, f32[512,256]{0,1:T(8,128)S(1)}, u32[]{:S(2)}, u32[]{:S(2)}) collective-permute-start(f32[512,256]{0,1:T(8,128)S(1)} %bitcast.24), channel_id=1, source_target_pairs={{4,0},{6,2},{8,4},{10,6},{12,8},{14,10},{0,12},{2,14},{5,1},{7,3},... | collective-permute-start | bytes 1572872 | tf_op jit(solution)/shard_map/ppermute | solution.py:17
  16.4 45.8 %collective-permute-start.2 = (f32[512,256]{0,1:T(8,128)S(1)}, f32[512,256]{0,1:T(8,128)S(1)}, u32[]{:S(2)}, u32[]{:S(2)}) collective-permute-start(f32[512,256]{0,1:T(8,128)S(1)} %bitcast.25), channel_id=1, source_target_pairs={{6,0},{8,2},{10,4},{12,6},{14,8},{0,10},{2,12},{4,14},{7,1},{9,3},... | collective-permute-start | bytes 1572872 | tf_op jit(solution)/shard_map/ppermute | solution.py:17
  16.7 46.3 %collective-permute-start.3 = (f32[512,256]{0,1:T(8,128)S(1)}, f32[512,256]{0,1:T(8,128)S(1)}, u32[]{:S(2)}, u32[]{:S(2)}) collective-permute-start(f32[512,256]{0,1:T(8,128)S(1)} %bitcast.26), channel_id=1, source_target_pairs={{8,0},{10,2},{12,4},{14,6},{0,8},{2,10},{4,12},{6,14},{9,1},{11,3}... | collective-permute-start | bytes 1572872 | tf_op jit(solution)/shard_map/ppermute | solution.py:17
  19.5 44.4 %collective-permute-start.4 = (f32[512,256]{0,1:T(8,128)S(1)}, f32[512,256]{0,1:T(8,128)S(1)}, u32[]{:S(2)}, u32[]{:S(2)}) collective-permute-start(f32[512,256]{0,1:T(8,128)S(1)} %bitcast.27), channel_id=1, source_target_pairs={{10,0},{12,2},{14,4},{0,6},{2,8},{4,10},{6,12},{8,14},{11,1},{13,3... | collective-permute-start | bytes 1572872 | tf_op jit(solution)/shard_map/ppermute | solution.py:17
  27.7 37.0 %collective-permute-start.5 = (f32[512,256]{0,1:T(8,128)S(1)}, f32[512,256]{0,1:T(8,128)S(1)}, u32[]{:S(2)}, u32[]{:S(2)}) collective-permute-start(f32[512,256]{0,1:T(8,128)S(1)} %bitcast.28), channel_id=1, source_target_pairs={{12,0},{14,2},{0,4},{2,6},{4,8},{6,10},{8,12},{10,14},{13,1},{15,3... | collective-permute-start | bytes 1572872 | tf_op jit(solution)/shard_map/ppermute | solution.py:17
  61.3 9.8 %collective-permute-start.6 = (f32[512,256]{0,1:T(8,128)S(1)}, f32[512,256]{0,1:T(8,128)S(1)}, u32[]{:S(2)}, u32[]{:S(2)}) collective-permute-start(f32[512,256]{0,1:T(8,128)S(1)} %bitcast.29), channel_id=1, source_target_pairs={{14,0},{0,2},{2,4},{4,6},{6,8},{8,10},{10,12},{12,14},{15,1},{1,3}... | collective-permute-start | bytes 1572872 | tf_op jit(solution)/shard_map/ppermute | solution.py:17
  77.0 80.4 %copy-start = (s32[8,32]{1,0:T(8,128)S(1)}, s32[8,32]{1,0:T(8,128)}, u32[]{:S(2)}) copy-start(s32[8,32]{1,0:T(8,128)} %param.9) | copy-start | bytes 3076
  153.0 188.7 %collective-permute-start.7 = (f32[512,1024]{1,0:T(8,128)}, f32[512,1024]{1,0:T(8,128)}, u32[]{:S(2)}, u32[]{:S(2)}) collective-permute-start(f32[512,1024]{1,0:T(8,128)} %fusion), channel_id=1, source_target_pairs={{0,1},{1,0},{2,3},{3,2},{4,5},{5,4},{6,7},{7,6},{8,9},{9,8},{10,11... | collective-permute-start | bytes 6291464 | tf_op jit(solution)/shard_map/ppermute | solution.py:42
Sparse Core Ops, SparseCore 0:
  10.4 124.6 all-gather.4
  136.8 204.8 all-gather.2

commit v4 on v2

v4 whole, which is shorter than its diff:
```python
import jax
import jax.numpy as jnp
from jax import lax
from jax.sharding import Mesh
from jax.sharding import PartitionSpec as P

BLOCK = 64
AXES = ("zl", "yh", "yl", "x", "core", "layer")
ROW = ("zl", "yh", "yl")
COL = ("x", "core")


def expand(block_mask):
    widened = jnp.repeat(block_mask.astype(jnp.float32), BLOCK, axis=-2)
    return jnp.repeat(widened, BLOCK, axis=-1)


def product_dot(a, b):
    return jnp.dot(a, b, precision=lax.Precision.HIGH, preferred_element_type=jnp.float32)


def gather_cols(block, index, n):
    parts = [block]
    for shift in range(1, n):
        parts.append(lax.ppermute(block, COL, [((i + shift) % n, i) for i in range(n)]))
    twice = jnp.concatenate(parts + parts, axis=1)
    return lax.dynamic_slice_in_dim(twice, (n - index) * block.shape[1], n * block.shape[1], axis=1)


def shards(density, dens_mask, hamiltonian, ham_mask, filter_mask, n_col):
    yl = lax.axis_index("yl")
    core = lax.axis_index("core")
    layer = lax.axis_index("layer")
    row = (lax.axis_index("zl") * 2 + lax.axis_index("yh")) * 2 + yl
    col = lax.axis_index("x") * 2 + core

    dens_vals = (density * expand(dens_mask))[0]
    ham_count = hamiltonian.shape[1]
    picked = lax.dynamic_slice_in_dim(ham_mask[0], row * (ham_count // BLOCK), ham_count // BLOCK, axis=0)
    ham_vals = hamiltonian[0] * expand(picked)
    half = ham_vals.shape[1] // 2
    kept = lax.dynamic_slice_in_dim(expand(filter_mask), layer * half, half, axis=1)

    pieces = {}
    for h in (0, 1):
        part = ham_vals[:, h * half:(h + 1) * half]
        for j in (0, 1):
            pieces[h, j] = lax.ppermute(part, ("yl", "core"), [(j * 2 + c, c * 2 + h) for c in (0, 1)])
    contrib = jnp.where(
        core == 0,
        jnp.concatenate([pieces[0, 0], pieces[0, 1]], axis=0),
        jnp.concatenate([pieces[1, 0], pieces[1, 1]], axis=0),
    )
    ham_own = lax.all_gather(contrib, ("zl", "yh"), axis=0, tiled=True)
    ham_other = lax.ppermute(ham_own, "core", [(0, 1), (1, 0)])

    dens_own = gather_cols(dens_vals, col, n_col)
    dens_nbr = lax.ppermute(dens_own, ("yl", "core"), [(0, 2), (3, 1)])
    dens_rows = jnp.where(core == yl, dens_own, dens_nbr)

    part_own = product_dot(dens_rows, ham_own)
    part_other = product_dot(dens_rows, ham_other)

    def route(value, target_layer):
        perm = []
        for j in (0, 1):
            for k in (0, 1):
                for src in (0, 1):
                    perm.append((j * 4 + k * 2 + src, k * 4 + j * 2 + target_layer(k)))
        return [
            lax.ppermute(value, ("yl", "core", "layer"), [p for p in perm if p[0] % 2 == src])
            for src in (0, 1)
        ]

    got = route(part_own, lambda k: k) + route(part_other, lambda k: 1 - k)
    total = (got[0] + got[1]) + (got[2] + got[3])
    return total * kept


def solution(mesh):
    rows, cols, layers = mesh.devices.shape
    fine = Mesh(mesh.devices.reshape(rows // 4, 2, 2, cols // 2, 2, layers), AXES)
    return jax.shard_map(
        lambda *args: shards(*args, cols),
        mesh=fine,
        in_specs=(
            P("layer", ROW, COL),
            P("layer", ROW, COL),
            P("layer", ROW, COL),
            P("layer", None, COL),
            P(ROW, COL),
        ),
        out_specs=P(ROW, ("x", "core", "layer")),
        check_vma=False,
    )
```

time: 386 us -> 485 us (1.26)
  the two profiles are of different devices: /device:TPU:78 before, /device:TPU:24 now
where the time goes in v4:
time: 485 us; the launch traced here: 480 us
  waiting for transfers between devices  366 us (75%)
  matrix products  35.8 us (7%)
  starting transfers between devices  31.6 us (7%)
  local copies, waits for them, and re-layouts  22.2 us (5%)
  between operations  13.6 us (3%)
  other arithmetic  10.7 us (2%)
    all_gather x1, waiting for transfers between devices, shards(): ham_own = lax.all_gather(contrib, ('zl', 'yh'), axis=0, tiled=True)  176 us
    ppermute x4, waiting for transfers between devices, route(): lax.ppermute(value, ('yl', 'core', 'layer'), [p for p in perm if p[0] % 2...  78.8 us
    ppermute x7, waiting for transfers between devices, gather_cols(): lax.ppermute(block, COL, [((i + shift) % n, i) for i in range(n)])  53.4 us
    ppermute x1, waiting for transfers between devices, shards(): dens_nbr = lax.ppermute(dens_own, ('yl', 'core'), [(0, 2), (3, 1)])  49.2 us
    dot_general x2, matrix products, product_dot(): jnp.dot(a, b, precision=lax.Precision.HIGH, preferred_element_type=jnp.fl...  35.8 us
    unnamed x23, local copies, waits for them, and re-layouts  15.3 us
    ppermute x4, starting transfers between devices, route(): lax.ppermute(value, ('yl', 'core', 'layer'), [p for p in perm if p[0] % 2...  14.8 us
  transfers between devices with their start and end apart: 18, of which 10 were waited for; matrix products, arithmetic and copies ran while one was open for 12% of the time, Pallas kernels for 0%

profile of v4, /device:TPU:24, one launch (start us, length us, event | category | flops | bytes accessed | tf_op | source)
XLA Modules:
  0.0 479.9 jit_solution(13155475771516272750)
XLA Ops:
  6.5 0.8 convert_bitcast_fusion.1
  7.6 1.6 copy.8
  9.3 0.7 collective-permute-start.10
  10.0 4.3 collective-permute-start.11
  14.3 1.3 collective-permute-start.8
  15.6 1.9 collective-permute-start.9
  17.6 3.4 collective-permute-done.11
  21.0 3.9 collective-permute-done.8
  24.8 1.8 collective-permute-done.9
  26.6 2.1 maximum_select_fusion
  28.7 175.5 %all-gather.2.cloned.1.call-done = f32[2048,1024]{0,1:T(8,128)} async-done(((f32[256,1024]{0,1:T(8,128)}), f32[2048,1024]{0,1:T(8,128)}) %all-gather.2.cloned.1.call-update) | async-done | bytes 8388624 | tf_op jit(solution)/shard_map/all_gather | solution.py:54
  204.7 1.0 constant_dynamic-update-slice_fusion.15
  205.6 2.8 collective-permute-start
  208.4 0.9 collective-permute-start.1
  209.3 2.4 collective-permute-start.3
  211.7 9.1 %collective-permute-done = f32[512,256]{0,1:T(8,128)S(1)} collective-permute-done((f32[512,256]{0,1:T(8,128)S(1)}, f32[512,256]{0,1:T(8,128)S(1)}, u32[]{:S(2)}, u32[]{:S(2)}) %collective-permute-start) | collective-permute-done | bytes 524320 | tf_op jit(solution)/shard_map/ppermute | solution.py:25
  220.7 1.0 collective-permute-start.4
  221.7 32.2 %collective-permute-done.1 = f32[512,256]{0,1:T(8,128)S(1)} collective-permute-done((f32[512,256]{0,1:T(8,128)S(1)}, f32[512,256]{0,1:T(8,128)S(1)}, u32[]{:S(2)}, u32[]{:S(2)}) %collective-permute-start.1) | collective-permute-done | bytes 524320 | tf_op jit(solution)/shard_map/ppermute | solution.py:25
  253.9 0.8 constant_dynamic-update-slice_fusion.14
  254.7 0.8 constant_dynamic-update-slice_fusion.13
  255.6 0.8 constant_dynamic-update-slice_fusion.12
  256.4 0.8 constant_dynamic-update-slice_fusion.11
  257.2 0.8 constant_dynamic-update-slice_fusion.10
  258.1 12.1 %collective-permute-done.5 = f32[512,256]{0,1:T(8,128)S(1)} collective-permute-done((f32[512,256]{0,1:T(8,128)S(1)}, f32[512,256]{0,1:T(8,128)S(1)}, u32[]{:S(2)}, u32[]{:S(2)}) %collective-permute-start.5) | collective-permute-done | bytes 524320 | tf_op jit(solution)/shard_map/ppermute | solution.py:25
  270.2 0.8 constant_dynamic-update-slice_fusion.9
  271.0 0.8 constant_dynamic-update-slice_fusion.8
  271.8 0.8 constant_dynamic-update-slice_fusion.7
  272.7 0.8 constant_dynamic-update-slice_fusion.6
  273.5 0.8 constant_dynamic-update-slice_fusion.5
  274.4 0.9 constant_dynamic-update-slice_fusion.4
  275.2 0.8 constant_dynamic-update-slice_fusion.3
  276.1 0.8 constant_dynamic-update-slice_fusion.2
  276.9 0.8 constant_dynamic-update-slice_fusion.1
  277.7 0.9 constant_dynamic-update-slice_fusion
  278.6 4.6 constant_dynamic-slice_fusion.1
  283.2 1.5 collective-permute-start.7
  284.7 49.2 %collective-permute-done.7 = f32[512,2048]{0,1:T(8,128)} collective-permute-done((f32[512,2048]{0,1:T(8,128)}, f32[512,2048]{0,1:T(8,128)}, u32[]{:S(2)}, u32[]{:S(2)}) %collective-permute-start.7) | collective-permute-done | bytes 4194336 | tf_op jit(solution)/shard_map/ppermute | solution.py:58
  333.9 17.9 %fusion.1 = f32[512,1024]{1,0:T(8,128)} fusion(f32[2048,1024]{0,1:T(8,128)} %all-gather.2.cloned.1.call-done, f32[512,2048]{0,1:T(8,128)} %constant_dynamic-slice_fusion.1, f32[512,2048]{0,1:T(8,128)} %collective-permute-done.7, pred[]{:T(512)S(6)} %eq.6), kind=kOutput, calls=%fused_computation.3 | convolution fusion | flops 6443499520 | bytes 18874368 | tf_op jit(solution)/shard_map/dot_general | solution.py:19
  351.9 2.8 collective-permute-start.12
  354.6 2.0 collective-permute-start.13
  356.6 17.9 %fusion = f32[512,1024]{1,0:T(8,128)} fusion(f32[2048,1024]{0,1:T(8,128)} %collective-permute-done.14, f32[512,2048]{0,1:T(8,128)} %constant_dynamic-slice_fusion.1, f32[512,2048]{0,1:T(8,128)} %collective-permute-done.7, pred[]{:T(512)S(6)} %eq.6), kind=kOutput, calls=%fused_computation.2 | convolution fusion | flops 6443499520 | bytes 18874368 | tf_op jit(solution)/shard_map/dot_general | solution.py:19
  374.5 8.7 %collective-permute-start.15 = (f32[512,1024]{1,0:T(8,128)}, f32[512,1024]{1,0:T(8,128)}, u32[]{:S(2)}, u32[]{:S(2)}) collective-permute-start(f32[512,1024]{1,0:T(8,128)} %fusion), channel_id=1, source_target_pairs={{0,1},{2,16},{16,3},{18,18},{4,5},{6,20},{20,7},{22,22},{8,9},{10,... | collective-permute-start | bytes 6291464 | tf_op jit(solution)/shard_map/ppermute | solution.py:71
  383.3 1.3 collective-permute-start.16
  384.9 0.5 broadcast_in_dim.29
  385.6 1.8 copy.12
  387.4 57.5 %collective-permute-done.15 = f32[512,1024]{1,0:T(8,128)} collective-permute-done((f32[512,1024]{1,0:T(8,128)}, f32[512,1024]{1,0:T(8,128)}, u32[]{:S(2)}, u32[]{:S(2)}) %collective-permute-start.15) | collective-permute-done | bytes 2097184 | tf_op jit(solution)/shard_map/ppermute | solution.py:71
  444.9 21.2 %collective-permute-done.16 = f32[512,1024]{1,0:T(8,128)} collective-permute-done((f32[512,1024]{1,0:T(8,128)}, f32[512,1024]{1,0:T(8,128)}, u32[]{:S(2)}, u32[]{:S(2)}) %collective-permute-start.16) | collective-permute-done | bytes 2097184 | tf_op jit(solution)/shard_map/ppermute | solution.py:71
  466.2 6.8 %add_multiply_fusion = f32[512,1024]{1,0:T(8,128)} fusion(f32[512,1024]{1,0:T(8,128)} %copy.12, f32[512,1024]{1,0:T(8,128)} %collective-permute-done.15, f32[512,1024]{1,0:T(8,128)} %collective-permute-done.16, f32[512,1024]{1,0:T(8,128)} %collective-permute-done.12, f32[512,1024]{1,0:T(8,128)} %collective-permute-done.13), kind=kLoop, calls=%fused_computation | loop fusion | flops 2097152 | bytes 12582912 | tf_op jit(solution)/shard_map/mul | solution.py:77
  (34 shorter events, 1.3 us)
Async XLA Ops:
  6.5 197.7 %copy-start = (f32[1,512,256]{2,1,0:T(8,128)S(1)}, f32[1,512,256]{2,1,0:T(8,128)}, u32[]{:S(2)}) copy-start(f32[1,512,256]{2,1,0:T(8,128)} %param.5) | copy-start | bytes 1572868
  6.5 197.9 %copy-start.2 = (s32[1,8,4]{1,2,0:T(4,128)S(1)}, s32[1,8,4]{1,2,0:T(4,128)}, u32[]{:S(2)}) copy-start(s32[1,8,4]{1,2,0:T(4,128)} %param.6) | copy-start | bytes 388
  6.5 197.7 %all-gather.2.cloned.1.call-start = ((), (), s32[]{:S(2)}) async-start(), calls=%async_computation | async-start | bytes 9437184 | tf_op jit(solution)/shard_map/all_gather | solution.py:54
  9.3 8.3 %collective-permute-start.10 = (f32[128,1024]{0,1:T(8,128)S(1)}, f32[128,1024]{0,1:T(8,128)S(1)}, u32[]{:S(2)}, u32[]{:S(2)}) collective-permute-start(f32[128,1024]{0,1:T(8,128)S(1)} %get-tuple-element.5), channel_id=1, source_target_pairs={{0,2},{2,18},{1,3},{3,19},{4,6},{6,22},{5,7},{7,23},{8,10},{10,26}... | collective-permute-start | bytes 1572872 | tf_op jit(solution)/shard_map/ppermute | solution.py:48
  10.0 11.0 %collective-permute-start.11 = (f32[128,1024]{0,1:T(8,128)S(1)}, f32[128,1024]{0,1:T(8,128)S(1)}, u32[]{:S(2)}, u32[]{:S(2)}) collective-permute-start(f32[128,1024]{0,1:T(8,128)S(1)} %get-tuple-element.5), channel_id=1, source_target_pairs={{16,2},{18,18},{17,3},{19,19},{20,6},{22,22},{21,7},{23,23},{24,10... | collective-permute-start | bytes 1572872 | tf_op jit(solution)/shard_map/ppermute | solution.py:48
  14.3 10.5 %collective-permute-start.8 = (f32[128,1024]{0,1:T(8,128)S(1)}, f32[128,1024]{0,1:T(8,128)S(1)}, u32[]{:S(2)}, u32[]{:S(2)}) collective-permute-start(f32[128,1024]{0,1:T(8,128)S(1)} %get-tuple-element.6), channel_id=1, source_target_pairs={{0,0},{2,16},{1,1},{3,17},{4,4},{6,20},{5,5},{7,21},{8,8},{10,24},... | collective-permute-start | bytes 1572872 | tf_op jit(solution)/shard_map/ppermute | solution.py:48
  15.6 11.0 %collective-permute-start.9 = (f32[128,1024]{0,1:T(8,128)S(1)}, f32[128,1024]{0,1:T(8,128)}, u32[]{:S(2)}, u32[]{:S(2)}) collective-permute-start(f32[128,1024]{0,1:T(8,128)S(1)} %get-tuple-element.6), channel_id=1, source_target_pairs={{16,0},{18,16},{17,1},{19,17},{20,4},{22,20},{21,5},{23,21},{24,8}... | collective-permute-start | bytes 1572872 | tf_op jit(solution)/shard_map/ppermute | solution.py:48
  204.3 152.4 %collective-permute-start.14 = (f32[2048,1024]{0,1:T(8,128)}, f32[2048,1024]{0,1:T(8,128)}, u32[]{:S(2)}, u32[]{:S(2)}) collective-permute-start(f32[2048,1024]{0,1:T(8,128)} %all-gather.2.cloned.1.call-done), channel_id=1, source_target_pairs={{0,2},{2,0},{1,3},{3,1},{4,6},{6,4},{5,7},{7,5},{8,10},{10,8},{9,1... | collective-permute-start | bytes 25165832 | tf_op jit(solution)/shard_map/ppermute | solution.py:55
  205.6 15.1 %collective-permute-start = (f32[512,256]{0,1:T(8,128)S(1)}, f32[512,256]{0,1:T(8,128)S(1)}, u32[]{:S(2)}, u32[]{:S(2)}) collective-permute-start(f32[512,256]{0,1:T(8,128)S(1)} %bitcast.23), channel_id=1, source_target_pairs={{2,0},{4,2},{6,4},{8,6},{10,8},{12,10},{14,12},{0,14},{3,1},{5,3},... | collective-permute-start | bytes 1572872 | tf_op jit(solution)/shard_map/ppermute | solution.py:25
  208.4 45.5 %collective-permute-start.1 = (f32[512,256]{0,1:T(8,128)S(1)}, f32[512,256]{0,1:T(8,128)S(1)}, u32[]{:S(2)}, u32[]{:S(2)}) collective-permute-start(f32[512,256]{0,1:T(8,128)S(1)} %bitcast.24), channel_id=1, source_target_pairs={{4,0},{6,2},{8,4},{10,6},{12,8},{14,10},{0,12},{2,14},{5,1},{7,3},... | collective-permute-start | bytes 1572872 | tf_op jit(solution)/shard_map/ppermute | solution.py:25
  209.3 45.5 %collective-permute-start.2 = (f32[512,256]{0,1:T(8,128)S(1)}, f32[512,256]{0,1:T(8,128)S(1)}, u32[]{:S(2)}, u32[]{:S(2)}) collective-permute-start(f32[512,256]{0,1:T(8,128)S(1)} %bitcast.25), channel_id=1, source_target_pairs={{6,0},{8,2},{10,4},{12,6},{14,8},{0,10},{2,12},{4,14},{7,1},{9,3},... | collective-permute-start | bytes 1572872 | tf_op jit(solution)/shard_map/ppermute | solution.py:25
  209.3 47.1 %collective-permute-start.3 = (f32[512,256]{0,1:T(8,128)S(1)}, f32[512,256]{0,1:T(8,128)S(1)}, u32[]{:S(2)}, u32[]{:S(2)}) collective-permute-start(f32[512,256]{0,1:T(8,128)S(1)} %bitcast.26), channel_id=1, source_target_pairs={{8,0},{10,2},{12,4},{14,6},{0,8},{2,10},{4,12},{6,14},{9,1},{11,3}... | collective-permute-start | bytes 1572872 | tf_op jit(solution)/shard_map/ppermute | solution.py:25
  220.7 36.5 %collective-permute-start.4 = (f32[512,256]{0,1:T(8,128)S(1)}, f32[512,256]{0,1:T(8,128)S(1)}, u32[]{:S(2)}, u32[]{:S(2)}) collective-permute-start(f32[512,256]{0,1:T(8,128)S(1)} %bitcast.27), channel_id=1, source_target_pairs={{10,0},{12,2},{14,4},{0,6},{2,8},{4,10},{6,12},{8,14},{11,1},{13,3... | collective-permute-start | bytes 1572872 | tf_op jit(solution)/shard_map/ppermute | solution.py:25
  253.9 16.3 %collective-permute-start.5 = (f32[512,256]{0,1:T(8,128)S(1)}, f32[512,256]{0,1:T(8,128)S(1)}, u32[]{:S(2)}, u32[]{:S(2)}) collective-permute-start(f32[512,256]{0,1:T(8,128)S(1)} %bitcast.28), channel_id=1, source_target_pairs={{12,0},{14,2},{0,4},{2,6},{4,8},{6,10},{8,12},{10,14},{13,1},{15,3... | collective-permute-start | bytes 1572872 | tf_op jit(solution)/shard_map/ppermute | solution.py:25
  254.7 16.3 %collective-permute-start.6 = (f32[512,256]{0,1:T(8,128)S(1)}, f32[512,256]{0,1:T(8,128)S(1)}, u32[]{:S(2)}, u32[]{:S(2)}) collective-permute-start(f32[512,256]{0,1:T(8,128)S(1)} %bitcast.29), channel_id=1, source_target_pairs={{14,0},{0,2},{2,4},{4,6},{6,8},{8,10},{10,12},{12,14},{15,1},{1,3}... | collective-permute-start | bytes 1572872 | tf_op jit(solution)/shard_map/ppermute | solution.py:25
  283.2 50.7 %collective-permute-start.7 = (f32[512,2048]{0,1:T(8,128)}, f32[512,2048]{0,1:T(8,128)}, u32[]{:S(2)}, u32[]{:S(2)}) collective-permute-start(f32[512,2048]{0,1:T(8,128)} %constant_dynamic-slice_fusion.1), channel_id=1, source_target_pairs={{0,16},{18,2},{1,17},{19,3},{4,20},{22,6},{5,21},{23,7},{8,24},{26... | collective-permute-start | bytes 12582920 | tf_op jit(solution)/shard_map/ppermute | solution.py:58
  351.9 32.8 %copy-start.1 = (s32[8,32]{1,0:T(8,128)S(1)}, s32[8,32]{1,0:T(8,128)}, u32[]{:S(2)}) copy-start(s32[8,32]{1,0:T(8,128)} %param.9) | copy-start | bytes 3076
  351.9 35.6 %collective-permute-start.12 = (f32[512,1024]{1,0:T(8,128)}, f32[512,1024]{1,0:T(8,128)}, u32[]{:S(2)}, u32[]{:S(2)}) collective-permute-start(f32[512,1024]{1,0:T(8,128)} %fusion.1), channel_id=1, source_target_pairs={{0,0},{2,17},{16,2},{18,19},{4,4},{6,21},{20,6},{22,23},{8,8},{10,... | collective-permute-start | bytes 6291464 | tf_op jit(solution)/shard_map/ppermute | solution.py:71
  354.6 32.8 %collective-permute-start.13 = (f32[512,1024]{1,0:T(8,128)}, f32[512,1024]{1,0:T(8,128)}, u32[]{:S(2)}, u32[]{:S(2)}) collective-permute-start(f32[512,1024]{1,0:T(8,128)} %fusion.1), channel_id=1, source_target_pairs={{1,0},{3,17},{17,2},{19,19},{5,4},{7,21},{21,6},{23,23},{9,8},{11,... | collective-permute-start | bytes 6291464 | tf_op jit(solution)/shard_map/ppermute | solution.py:71
  374.5 70.4 %collective-permute-start.15 = (f32[512,1024]{1,0:T(8,128)}, f32[512,1024]{1,0:T(8,128)}, u32[]{:S(2)}, u32[]{:S(2)}) collective-permute-start(f32[512,1024]{1,0:T(8,128)} %fusion), channel_id=1, source_target_pairs={{0,1},{2,16},{16,3},{18,18},{4,5},{6,20},{20,7},{22,22},{8,9},{10,... | collective-permute-start | bytes 6291464 | tf_op jit(solution)/shard_map/ppermute | solution.py:71
  383.3 82.9 %collective-permute-start.16 = (f32[512,1024]{1,0:T(8,128)}, f32[512,1024]{1,0:T(8,128)}, u32[]{:S(2)}, u32[]{:S(2)}) collective-permute-start(f32[512,1024]{1,0:T(8,128)} %fusion), channel_id=1, source_target_pairs={{1,1},{3,16},{17,3},{19,18},{5,5},{7,20},{21,7},{23,22},{9,9},{11,... | collective-permute-start | bytes 6291464 | tf_op jit(solution)/shard_map/ppermute | solution.py:71
Sparse Core Ops, SparseCore 0:
  28.9 175.3 all-gather.1

commit v5 on v3

--- a/solution.py
+++ b/solution.py
@@ -37,11 +37,10 @@
 
     send_half = lax.dynamic_slice_in_dim(ham_vals, (1 - layer) * half, half, axis=1)
     keep_half = lax.dynamic_slice_in_dim(ham_vals, layer * half, half, axis=1)
-    ham_send = lax.all_gather(send_half, "row", axis=0, tiled=True)
+    ham_panel = lax.all_gather(jnp.concatenate([send_half, keep_half], axis=1), "row", axis=0, tiled=True)
     dens_row = gather_cols(dens_vals, "col", n_col)
-    received = lax.ppermute(product_dot(dens_row, ham_send), "layer", [(0, 1), (1, 0)])
-    ham_keep = lax.all_gather(keep_half, "row", axis=0, tiled=True)
-    own = product_dot(dens_row, ham_keep)
+    received = lax.ppermute(product_dot(dens_row, ham_panel[:, :half]), "layer", [(0, 1), (1, 0)])
+    own = lax.optimization_barrier(product_dot(dens_row, ham_panel[:, half:]))
     return (own + received) * kept
 
 

time: 368 us -> 334 us (0.908)
  the two profiles are of different devices: /device:TPU:64 before, /device:TPU:24 now
where the time goes in v5:
time: 334 us; the launch traced here: 333 us
  waiting for transfers between devices  251 us (75%)
  matrix products  35.2 us (11%)
  local copies, waits for them, and re-layouts  17.7 us (5%)
  between operations  13.5 us (4%)
  starting transfers between devices  9.23 us (3%)
  other arithmetic  6.38 us (2%)
    all_gather x1, waiting for transfers between devices, shards(): lax.all_gather(jnp.concatenate([send_half, keep_half], axis=1), 'row', ax...  138 us
    ppermute x1, waiting for transfers between devices, shards(): lax.ppermute(product_dot(dens_row, ham_panel[:, :half]), 'layer', [(0, 1)...  66.4 us
    ppermute x7, waiting for transfers between devices, gather_cols(): lax.ppermute(block, axis_name, [((i + shift) % n, i) for i in range(n)])  46.6 us
    dot_general x2, matrix products, product_dot(): jnp.dot(a, b, precision=lax.Precision.HIGH, preferred_element_type=jnp.fl...  35.2 us
    unnamed x25, local copies, waits for them, and re-layouts  15.4 us
  transfers between devices with their start and end apart: 9, of which 5 were waited for; matrix products, arithmetic and copies ran while one was open for 10% of the time, Pallas kernels for 0%

profile of v5, /device:TPU:24, one launch (start us, length us, event | category | flops | bytes accessed | tf_op | source)
XLA Modules:
  0.0 333.4 jit_solution(9912292531895205715)
XLA Ops:
  6.5 0.8 fusion.9
  7.3 0.1 copy.9
  7.4 0.1 broadcast_in_dim.26
  7.5 0.1 reshape.23
  7.6 1.6 copy.8
  9.1 0.1 bitcast_multiply_fusion
  9.2 0.1 constant_dynamic-slice_fusion.2
  9.3 1.0 pad_maximum_fusion
  10.3 0.0 all-gather.2.cloned.1.call-update
  10.4 0.2 copy.7
  10.6 0.1 broadcast_in_dim.22
  10.7 0.1 broadcast_in_dim.23
  10.7 0.9 constant_dynamic-update-slice_fusion.15
  11.7 2.2 collective-permute-start
  13.9 0.8 collective-permute-start.1
  14.7 0.4 collective-permute-start.2
  15.1 2.7 collective-permute-start.3
  17.8 0.0 collective-permute-start.4
  17.8 8.3 %collective-permute-done = f32[512,256]{0,1:T(8,128)S(1)} collective-permute-done((f32[512,256]{0,1:T(8,128)S(1)}, f32[512,256]{0,1:T(8,128)S(1)}, u32[]{:S(2)}, u32[]{:S(2)}) %collective-permute-start) | collective-permute-done | bytes 524320 | tf_op jit(solution)/shard_map/ppermute | solution.py:17
  26.1 0.8 constant_dynamic-update-slice_fusion.14
  26.9 32.7 %collective-permute-done.1 = f32[512,256]{0,1:T(8,128)S(1)} collective-permute-done((f32[512,256]{0,1:T(8,128)S(1)}, f32[512,256]{0,1:T(8,128)S(1)}, u32[]{:S(2)}, u32[]{:S(2)}) %collective-permute-start.1) | collective-permute-done | bytes 524320 | tf_op jit(solution)/shard_map/ppermute | solution.py:17
  59.7 0.9 constant_dynamic-update-slice_fusion.13
  60.5 0.8 constant_dynamic-update-slice_fusion.12
  61.4 0.9 constant_dynamic-update-slice_fusion.11
  62.2 0.8 constant_dynamic-update-slice_fusion.10
  63.1 0.8 constant_dynamic-update-slice_fusion.9
  63.9 5.6 %collective-permute-done.6 = f32[512,256]{0,1:T(8,128)S(1)} collective-permute-done((f32[512,256]{0,1:T(8,128)S(1)}, f32[512,256]{0,1:T(8,128)S(1)}, u32[]{:S(2)}, u32[]{:S(2)}) %collective-permute-start.6) | collective-permute-done | bytes 524320 | tf_op jit(solution)/shard_map/ppermute | solution.py:17
  69.5 0.8 constant_dynamic-update-slice_fusion.8
  70.3 0.8 constant_dynamic-update-slice_fusion.7
  71.2 0.8 constant_dynamic-update-slice_fusion.6
  72.0 0.9 constant_dynamic-update-slice_fusion.5
  72.9 0.9 constant_dynamic-update-slice_fusion.4
  73.7 0.8 constant_dynamic-update-slice_fusion.3
  74.5 0.8 constant_dynamic-update-slice_fusion.2
  75.4 0.8 constant_dynamic-update-slice_fusion.1
  76.2 0.9 constant_dynamic-update-slice_fusion
  77.1 138.3 %all-gather.2.cloned.1.call-done = f32[2048,2048]{0,1:T(8,128)} async-done(((f32[128,2048]{0,1:T(8,128)}), f32[2048,2048]{0,1:T(8,128)}) %all-gather.2.cloned.1.call-update) | async-done | bytes 16777232 | tf_op jit(solution)/shard_map/all_gather | solution.py:40
  215.4 17.9 %fusion = f32[512,1024]{1,0:T(8,128)} fusion(f32[2048,2048]{0,1:T(8,128)} %all-gather.2.cloned.1.call-done, f32[512,4096]{0,1:T(8,128)} %constant_dynamic-update-slice_fusion, s32[]{:T(128)S(6)} %select_n.13), kind=kOutput, calls=%fused_computation | convolution fusion | flops 6442450944 | bytes 14680068 | tf_op jit(solution)/shard_map/dot_general | solution.py:24
  233.3 3.1 collective-permute-start.7
  236.4 0.1 copy.10
  236.5 0.1 broadcast_in_dim.28
  236.6 0.1 reshape.25
  236.7 0.5 broadcast_in_dim.29
  237.2 0.2 constant_dynamic-slice_fusion
  237.4 1.8 copy.12
  239.2 17.3 %fusion.2 = f32[512,1024]{1,0:T(8,128)S(1)} fusion(f32[2048,2048]{0,1:T(8,128)} %all-gather.2.cloned.1.call-done, f32[512,4096]{0,1:T(8,128)} %constant_dynamic-update-slice_fusion, s32[]{:T(128)S(6)} %select_n.13), kind=kOutput, calls=%fused_computation.2 | convolution fusion | flops 6442450944 | bytes 14680068 | tf_op jit(solution)/shard_map/dot_general | solution.py:24
  256.5 66.4 %collective-permute-done.7 = f32[512,1024]{1,0:T(8,128)} collective-permute-done((f32[512,1024]{1,0:T(8,128)}, f32[512,1024]{1,0:T(8,128)}, u32[]{:S(2)}, u32[]{:S(2)}) %collective-permute-start.7) | collective-permute-done | bytes 2097184 | tf_op jit(solution)/shard_map/ppermute | solution.py:42
  323.0 3.6 %add_multiply_fusion = f32[512,1024]{1,0:T(8,128)} fusion(f32[512,1024]{1,0:T(8,128)S(1)} %copy-done, f32[512,1024]{1,0:T(8,128)S(1)} %fusion.2, f32[512,1024]{1,0:T(8,128)} %collective-permute-done.7), kind=kLoop, calls=%fused_computation.6 | loop fusion | flops 1048576 | bytes 8388608 | tf_op jit(solution)/shard_map/mul | solution.py:44
  (17 shorter events, 0.0 us)
Async XLA Ops:
  6.5 3.8 %copy-start.1 = (f32[1,512,256]{2,1,0:T(8,128)S(1)}, f32[1,512,256]{2,1,0:T(8,128)}, u32[]{:S(2)}) copy-start(f32[1,512,256]{2,1,0:T(8,128)} %param.5) | copy-start | bytes 1572868
  6.5 4.0 %copy-start.3 = (s32[1,8,4]{1,2,0:T(4,128)S(1)}, s32[1,8,4]{1,2,0:T(4,128)}, u32[]{:S(2)}) copy-start(s32[1,8,4]{1,2,0:T(4,128)} %param.6) | copy-start | bytes 388
  6.5 208.9 %all-gather.2.cloned.1.call-start = ((), (), s32[]{:S(2)}) async-start(), calls=%async_computation | async-start | bytes 17825792 | tf_op jit(solution)/shard_map/all_gather | solution.py:40
  11.7 14.4 %collective-permute-start = (f32[512,256]{0,1:T(8,128)S(1)}, f32[512,256]{0,1:T(8,128)S(1)}, u32[]{:S(2)}, u32[]{:S(2)}) collective-permute-start(f32[512,256]{0,1:T(8,128)S(1)} %bitcast.21), channel_id=1, source_target_pairs={{2,0},{4,2},{6,4},{8,6},{10,8},{12,10},{14,12},{0,14},{3,1},{5,3},... | collective-permute-start | bytes 1572872 | tf_op jit(solution)/shard_map/ppermute | solution.py:17
  13.9 45.8 %collective-permute-start.1 = (f32[512,256]{0,1:T(8,128)S(1)}, f32[512,256]{0,1:T(8,128)S(1)}, u32[]{:S(2)}, u32[]{:S(2)}) collective-permute-start(f32[512,256]{0,1:T(8,128)S(1)} %bitcast.22), channel_id=1, source_target_pairs={{4,0},{6,2},{8,4},{10,6},{12,8},{14,10},{0,12},{2,14},{5,1},{7,3},... | collective-permute-start | bytes 1572872 | tf_op jit(solution)/shard_map/ppermute | solution.py:17
  14.7 45.8 %collective-permute-start.2 = (f32[512,256]{0,1:T(8,128)S(1)}, f32[512,256]{0,1:T(8,128)S(1)}, u32[]{:S(2)}, u32[]{:S(2)}) collective-permute-start(f32[512,256]{0,1:T(8,128)S(1)} %bitcast.23), channel_id=1, source_target_pairs={{6,0},{8,2},{10,4},{12,6},{14,8},{0,10},{2,12},{4,14},{7,1},{9,3},... | collective-permute-start | bytes 1572872 | tf_op jit(solution)/shard_map/ppermute | solution.py:17
  15.1 46.3 %collective-permute-start.3 = (f32[512,256]{0,1:T(8,128)S(1)}, f32[512,256]{0,1:T(8,128)S(1)}, u32[]{:S(2)}, u32[]{:S(2)}) collective-permute-start(f32[512,256]{0,1:T(8,128)S(1)} %bitcast.24), channel_id=1, source_target_pairs={{8,0},{10,2},{12,4},{14,6},{0,8},{2,10},{4,12},{6,14},{9,1},{11,3}... | collective-permute-start | bytes 1572872 | tf_op jit(solution)/shard_map/ppermute | solution.py:17
  17.8 44.4 %collective-permute-start.4 = (f32[512,256]{0,1:T(8,128)S(1)}, f32[512,256]{0,1:T(8,128)S(1)}, u32[]{:S(2)}, u32[]{:S(2)}) collective-permute-start(f32[512,256]{0,1:T(8,128)S(1)} %bitcast.25), channel_id=1, source_target_pairs={{10,0},{12,2},{14,4},{0,6},{2,8},{4,10},{6,12},{8,14},{11,1},{13,3... | collective-permute-start | bytes 1572872 | tf_op jit(solution)/shard_map/ppermute | solution.py:17
  26.1 37.0 %collective-permute-start.5 = (f32[512,256]{0,1:T(8,128)S(1)}, f32[512,256]{0,1:T(8,128)S(1)}, u32[]{:S(2)}, u32[]{:S(2)}) collective-permute-start(f32[512,256]{0,1:T(8,128)S(1)} %bitcast.26), channel_id=1, source_target_pairs={{12,0},{14,2},{0,4},{2,6},{4,8},{6,10},{8,12},{10,14},{13,1},{15,3... | collective-permute-start | bytes 1572872 | tf_op jit(solution)/shard_map/ppermute | solution.py:17
  59.7 9.8 %collective-permute-start.6 = (f32[512,256]{0,1:T(8,128)S(1)}, f32[512,256]{0,1:T(8,128)S(1)}, u32[]{:S(2)}, u32[]{:S(2)}) collective-permute-start(f32[512,256]{0,1:T(8,128)S(1)} %bitcast.27), channel_id=1, source_target_pairs={{14,0},{0,2},{2,4},{4,6},{6,8},{8,10},{10,12},{12,14},{15,1},{1,3}... | collective-permute-start | bytes 1572872 | tf_op jit(solution)/shard_map/ppermute | solution.py:17
  75.4 161.1 %copy-start.2 = (s32[8,32]{1,0:T(8,128)S(1)}, s32[8,32]{1,0:T(8,128)}, u32[]{:S(2)}) copy-start(s32[8,32]{1,0:T(8,128)} %param.9) | copy-start | bytes 3076
  233.3 89.6 %collective-permute-start.7 = (f32[512,1024]{1,0:T(8,128)}, f32[512,1024]{1,0:T(8,128)}, u32[]{:S(2)}, u32[]{:S(2)}) collective-permute-start(f32[512,1024]{1,0:T(8,128)} %fusion), channel_id=1, source_target_pairs={{0,1},{1,0},{2,3},{3,2},{4,5},{5,4},{6,7},{7,6},{8,9},{9,8},{10,11... | collective-permute-start | bytes 6291464 | tf_op jit(solution)/shard_map/ppermute | solution.py:42
  239.2 83.7 %copy-start = (f32[512,1024]{1,0:T(8,128)S(1)}, f32[512,1024]{1,0:T(8,128)}, u32[]{:S(2)}) copy-start(f32[512,1024]{1,0:T(8,128)} %copy.12) | copy-start | bytes 6291460
Sparse Core Ops, SparseCore 0:
  10.5 204.8 all-gather.1

commit v6 on v5

--- a/solution.py
+++ b/solution.py
@@ -39,7 +39,14 @@
     keep_half = lax.dynamic_slice_in_dim(ham_vals, layer * half, half, axis=1)
     ham_panel = lax.all_gather(jnp.concatenate([send_half, keep_half], axis=1), "row", axis=0, tiled=True)
     dens_row = gather_cols(dens_vals, "col", n_col)
-    received = lax.ppermute(product_dot(dens_row, ham_panel[:, :half]), "layer", [(0, 1), (1, 0)])
+    step = half // 2
+    received = jnp.concatenate(
+        [
+            lax.ppermute(product_dot(dens_row, ham_panel[:, i:i + step]), "layer", [(0, 1), (1, 0)])
+            for i in range(0, half, step)
+        ],
+        axis=1,
+    )
     own = lax.optimization_barrier(product_dot(dens_row, ham_panel[:, half:]))
     return (own + received) * kept
 

time: 334 us -> 327 us (0.979)
  waiting for transfers between devices: 251 us -> 239 us
    ppermute x1 -> x2, waiting for transfers between devices: 66.4 us -> 53.6 us  [shards(): lax.ppermute(product_dot(dens_row, ham_panel[:, i:i + step]), 'layer', [(...]
    dot_general x2 -> x3, matrix products: 35.2 us -> 38.5 us  [product_dot(): jnp.dot(a, b, precision=lax.Precision.HIGH, preferred_element_type=jnp.fl...]
    unnamed x25 -> x27, local copies, waits for them, and re-layouts: 15.4 us -> 15.3 us
  transfers between devices with their start and end apart: 9 -> 10, of which waited for: 5 -> 6; matrix products, arithmetic and copies ran while one was open for 10% -> 13% of each run, Pallas kernels for 0% -> 0%
where the time goes in v6:
time: 327 us; the launch traced here: 326 us
  waiting for transfers between devices  239 us (73%)
  matrix products  38.5 us (12%)
  local copies, waits for them, and re-layouts  17.7 us (5%)
  between operations  13.5 us (4%)
  starting transfers between devices  12.1 us (4%)
  other arithmetic  6.03 us (2%)
    all_gather x1, waiting for transfers between devices, shards(): lax.all_gather(jnp.concatenate([send_half, keep_half], axis=1), 'row', ax...  138 us
    ppermute x2, waiting for transfers between devices, shards(): lax.ppermute(product_dot(dens_row, ham_panel[:, i:i + step]), 'layer', [(...  53.6 us
    ppermute x7, waiting for transfers between devices, gather_cols(): lax.ppermute(block, axis_name, [((i + shift) % n, i) for i in range(n)])  46.6 us
    dot_general x3, matrix products, product_dot(): jnp.dot(a, b, precision=lax.Precision.HIGH, preferred_element_type=jnp.fl...  38.5 us
    unnamed x27, local copies, waits for them, and re-layouts  15.3 us
  transfers between devices with their start and end apart: 10, of which 6 were waited for; matrix products, arithmetic and copies ran while one was open for 13% of the time, Pallas kernels for 0%

profile of v6, /device:TPU:24, one launch (start us, length us, event | category | flops | bytes accessed | tf_op | source)
XLA Modules:
  0.0 326.4 jit_solution(12159422148814183254)
XLA Ops:
  6.5 0.8 fusion.14
  7.3 0.1 copy.9
  7.4 0.1 broadcast_in_dim.26
  7.5 0.1 reshape.23
  7.6 1.6 copy.8
  9.1 0.1 bitcast_multiply_fusion
  9.2 0.1 constant_dynamic-slice_fusion.2
  9.3 1.0 pad_maximum_fusion
  10.4 0.2 copy.7
  10.7 0.1 broadcast_in_dim.23
  10.7 0.9 constant_dynamic-update-slice_fusion.15
  11.7 2.2 collective-permute-start
  13.9 0.8 collective-permute-start.1
  14.7 0.4 collective-permute-start.2
  15.1 2.7 collective-permute-start.3
  17.8 8.3 %collective-permute-done = f32[512,256]{0,1:T(8,128)S(1)} collective-permute-done((f32[512,256]{0,1:T(8,128)S(1)}, f32[512,256]{0,1:T(8,128)S(1)}, u32[]{:S(2)}, u32[]{:S(2)}) %collective-permute-start) | collective-permute-done | bytes 524320 | tf_op jit(solution)/shard_map/ppermute | solution.py:17
  26.1 0.8 constant_dynamic-update-slice_fusion.14
  26.9 32.7 %collective-permute-done.1 = f32[512,256]{0,1:T(8,128)S(1)} collective-permute-done((f32[512,256]{0,1:T(8,128)S(1)}, f32[512,256]{0,1:T(8,128)S(1)}, u32[]{:S(2)}, u32[]{:S(2)}) %collective-permute-start.1) | collective-permute-done | bytes 524320 | tf_op jit(solution)/shard_map/ppermute | solution.py:17
  59.7 0.9 constant_dynamic-update-slice_fusion.13
  60.5 0.8 constant_dynamic-update-slice_fusion.12
  61.4 0.8 constant_dynamic-update-slice_fusion.11
  62.2 0.8 constant_dynamic-update-slice_fusion.10
  63.1 0.8 constant_dynamic-update-slice_fusion.9
  63.9 5.6 %collective-permute-done.6 = f32[512,256]{0,1:T(8,128)S(1)} collective-permute-done((f32[512,256]{0,1:T(8,128)S(1)}, f32[512,256]{0,1:T(8,128)S(1)}, u32[]{:S(2)}, u32[]{:S(2)}) %collective-permute-start.6) | collective-permute-done | bytes 524320 | tf_op jit(solution)/shard_map/ppermute | solution.py:17
  69.5 0.8 constant_dynamic-update-slice_fusion.8
  70.3 0.8 constant_dynamic-update-slice_fusion.7
  71.2 0.8 constant_dynamic-update-slice_fusion.6
  72.0 0.9 constant_dynamic-update-slice_fusion.5
  72.9 0.8 constant_dynamic-update-slice_fusion.4
  73.7 0.8 constant_dynamic-update-slice_fusion.3
  74.5 0.8 constant_dynamic-update-slice_fusion.2
  75.4 0.8 constant_dynamic-update-slice_fusion.1
  76.2 0.9 constant_dynamic-update-slice_fusion
  77.1 138.3 %all-gather.2.cloned.1.call-done = f32[2048,2048]{0,1:T(8,128)} async-done(((f32[128,2048]{0,1:T(8,128)}), f32[2048,2048]{0,1:T(8,128)}) %all-gather.2.cloned.1.call-update) | async-done | bytes 16777232 | tf_op jit(solution)/shard_map/all_gather | solution.py:40
  215.4 11.3 %fusion.4 = f32[512,512]{1,0:T(8,128)} fusion(f32[2048,2048]{0,1:T(8,128)} %all-gather.2.cloned.1.call-done, f32[512,4096]{0,1:T(8,128)} %constant_dynamic-update-slice_fusion, s32[]{:T(128)S(6)} %select_n.13), kind=kOutput, calls=%fused_computation.4 | convolution fusion | flops 3221225472 | bytes 9437188 | tf_op jit(solution)/shard_map/dot_general | solution.py:24
  226.7 3.1 collective-permute-start.7
  229.8 10.0 %fusion.2 = f32[512,512]{1,0:T(8,128)} fusion(f32[2048,2048]{0,1:T(8,128)} %all-gather.2.cloned.1.call-done, f32[512,4096]{0,1:T(8,128)S(1)} %copy-done.2, s32[]{:T(128)S(6)} %select_n.13), kind=kOutput, calls=%fused_computation.2 | convolution fusion | flops 3221225472 | bytes 9437188 | tf_op jit(solution)/shard_map/dot_general | solution.py:24
  239.8 2.8 collective-permute-start.8
  242.6 0.1 copy.10
  242.7 0.1 broadcast_in_dim.28
  242.8 0.1 reshape.25
  242.9 0.5 broadcast_in_dim.29
  243.4 0.2 constant_dynamic-slice_fusion
  243.6 1.8 copy.12
  245.4 17.3 %fusion = f32[512,1024]{1,0:T(8,128)S(1)} fusion(f32[2048,2048]{0,1:T(8,128)} %all-gather.2.cloned.1.call-done, f32[512,4096]{0,1:T(8,128)} %constant_dynamic-update-slice_fusion, s32[]{:T(128)S(6)} %select_n.13), kind=kOutput, calls=%fused_computation | convolution fusion | flops 6442450944 | bytes 14680068 | tf_op jit(solution)/shard_map/dot_general | solution.py:24
  262.7 7.7 %collective-permute-done.7 = f32[512,512]{1,0:T(8,128)S(1)} collective-permute-done((f32[512,512]{1,0:T(8,128)}, f32[512,512]{1,0:T(8,128)S(1)}, u32[]{:S(2)}, u32[]{:S(2)}) %collective-permute-start.7) | collective-permute-done | bytes 1048608 | tf_op jit(solution)/shard_map/ppermute | solution.py:45
  270.3 46.0 %collective-permute-done.8 = f32[512,512]{1,0:T(8,128)} collective-permute-done((f32[512,512]{1,0:T(8,128)}, f32[512,512]{1,0:T(8,128)}, u32[]{:S(2)}, u32[]{:S(2)}) %collective-permute-start.8) | collective-permute-done | bytes 1048608 | tf_op jit(solution)/shard_map/ppermute | solution.py:45
  316.3 3.2 fusion.9
  (22 shorter events, 0.1 us)
Async XLA Ops:
  6.5 3.8 %copy-start.1 = (f32[1,512,256]{2,1,0:T(8,128)S(1)}, f32[1,512,256]{2,1,0:T(8,128)}, u32[]{:S(2)}) copy-start(f32[1,512,256]{2,1,0:T(8,128)} %param.5) | copy-start | bytes 1572868
  6.5 4.0 %copy-start.4 = (s32[1,8,4]{1,2,0:T(4,128)S(1)}, s32[1,8,4]{1,2,0:T(4,128)}, u32[]{:S(2)}) copy-start(s32[1,8,4]{1,2,0:T(4,128)} %param.6) | copy-start | bytes 388
  6.5 208.9 %all-gather.2.cloned.1.call-start = ((), (), s32[]{:S(2)}) async-start(), calls=%async_computation | async-start | bytes 17825792 | tf_op jit(solution)/shard_map/all_gather | solution.py:40
  11.7 14.4 %collective-permute-start = (f32[512,256]{0,1:T(8,128)S(1)}, f32[512,256]{0,1:T(8,128)S(1)}, u32[]{:S(2)}, u32[]{:S(2)}) collective-permute-start(f32[512,256]{0,1:T(8,128)S(1)} %bitcast.21), channel_id=1, source_target_pairs={{2,0},{4,2},{6,4},{8,6},{10,8},{12,10},{14,12},{0,14},{3,1},{5,3},... | collective-permute-start | bytes 1572872 | tf_op jit(solution)/shard_map/ppermute | solution.py:17
  13.9 45.8 %collective-permute-start.1 = (f32[512,256]{0,1:T(8,128)S(1)}, f32[512,256]{0,1:T(8,128)S(1)}, u32[]{:S(2)}, u32[]{:S(2)}) collective-permute-start(f32[512,256]{0,1:T(8,128)S(1)} %bitcast.22), channel_id=1, source_target_pairs={{4,0},{6,2},{8,4},{10,6},{12,8},{14,10},{0,12},{2,14},{5,1},{7,3},... | collective-permute-start | bytes 1572872 | tf_op jit(solution)/shard_map/ppermute | solution.py:17
  14.7 45.8 %collective-permute-start.2 = (f32[512,256]{0,1:T(8,128)S(1)}, f32[512,256]{0,1:T(8,128)S(1)}, u32[]{:S(2)}, u32[]{:S(2)}) collective-permute-start(f32[512,256]{0,1:T(8,128)S(1)} %bitcast.23), channel_id=1, source_target_pairs={{6,0},{8,2},{10,4},{12,6},{14,8},{0,10},{2,12},{4,14},{7,1},{9,3},... | collective-permute-start | bytes 1572872 | tf_op jit(solution)/shard_map/ppermute | solution.py:17
  15.1 46.3 %collective-permute-start.3 = (f32[512,256]{0,1:T(8,128)S(1)}, f32[512,256]{0,1:T(8,128)S(1)}, u32[]{:S(2)}, u32[]{:S(2)}) collective-permute-start(f32[512,256]{0,1:T(8,128)S(1)} %bitcast.24), channel_id=1, source_target_pairs={{8,0},{10,2},{12,4},{14,6},{0,8},{2,10},{4,12},{6,14},{9,1},{11,3}... | collective-permute-start | bytes 1572872 | tf_op jit(solution)/shard_map/ppermute | solution.py:17
  17.8 44.4 %collective-permute-start.4 = (f32[512,256]{0,1:T(8,128)S(1)}, f32[512,256]{0,1:T(8,128)S(1)}, u32[]{:S(2)}, u32[]{:S(2)}) collective-permute-start(f32[512,256]{0,1:T(8,128)S(1)} %bitcast.25), channel_id=1, source_target_pairs={{10,0},{12,2},{14,4},{0,6},{2,8},{4,10},{6,12},{8,14},{11,1},{13,3... | collective-permute-start | bytes 1572872 | tf_op jit(solution)/shard_map/ppermute | solution.py:17
  26.1 37.0 %collective-permute-start.5 = (f32[512,256]{0,1:T(8,128)S(1)}, f32[512,256]{0,1:T(8,128)S(1)}, u32[]{:S(2)}, u32[]{:S(2)}) collective-permute-start(f32[512,256]{0,1:T(8,128)S(1)} %bitcast.26), channel_id=1, source_target_pairs={{12,0},{14,2},{0,4},{2,6},{4,8},{6,10},{8,12},{10,14},{13,1},{15,3... | collective-permute-start | bytes 1572872 | tf_op jit(solution)/shard_map/ppermute | solution.py:17
  59.7 9.8 %collective-permute-start.6 = (f32[512,256]{0,1:T(8,128)S(1)}, f32[512,256]{0,1:T(8,128)S(1)}, u32[]{:S(2)}, u32[]{:S(2)}) collective-permute-start(f32[512,256]{0,1:T(8,128)S(1)} %bitcast.27), channel_id=1, source_target_pairs={{14,0},{0,2},{2,4},{4,6},{6,8},{8,10},{10,12},{12,14},{15,1},{1,3}... | collective-permute-start | bytes 1572872 | tf_op jit(solution)/shard_map/ppermute | solution.py:17
  77.1 165.5 %copy-start.3 = (s32[8,32]{1,0:T(8,128)S(1)}, s32[8,32]{1,0:T(8,128)}, u32[]{:S(2)}) copy-start(s32[8,32]{1,0:T(8,128)} %param.9) | copy-start | bytes 3076
  215.4 14.4 %copy-start.2 = (f32[512,4096]{0,1:T(8,128)S(1)}, f32[512,4096]{0,1:T(8,128)}, u32[]{:S(2)}) copy-start(f32[512,4096]{0,1:T(8,128)} %constant_dynamic-update-slice_fusion) | copy-start | bytes 25165828
  226.7 43.6 %collective-permute-start.7 = (f32[512,512]{1,0:T(8,128)}, f32[512,512]{1,0:T(8,128)S(1)}, u32[]{:S(2)}, u32[]{:S(2)}) collective-permute-start(f32[512,512]{1,0:T(8,128)} %fusion.4), channel_id=1, source_target_pairs={{0,1},{1,0},{2,3},{3,2},{4,5},{5,4},{6,7},{7,6},{8,9},{9,8},{10,11... | collective-permute-start | bytes 3145736 | tf_op jit(solution)/shard_map/ppermute | solution.py:45
  239.8 76.6 %collective-permute-start.8 = (f32[512,512]{1,0:T(8,128)}, f32[512,512]{1,0:T(8,128)}, u32[]{:S(2)}, u32[]{:S(2)}) collective-permute-start(f32[512,512]{1,0:T(8,128)} %fusion.2), channel_id=1, source_target_pairs={{0,1},{1,0},{2,3},{3,2},{4,5},{5,4},{6,7},{7,6},{8,9},{9,8},{10,11... | collective-permute-start | bytes 3145736 | tf_op jit(solution)/shard_map/ppermute | solution.py:45
  245.4 70.9 %copy-start = (f32[512,1024]{1,0:T(8,128)S(1)}, f32[512,1024]{1,0:T(8,128)}, u32[]{:S(2)}) copy-start(f32[512,1024]{1,0:T(8,128)} %copy.12) | copy-start | bytes 6291460
Sparse Core Ops, SparseCore 0:
  10.5 204.8 all-gather.1

commit v7 on v6

--- a/solution.py
+++ b/solution.py
@@ -12,12 +12,13 @@
 
 
 def gather_cols(block, axis_name, n):
-    parts = [block]
-    for shift in range(1, n):
-        parts.append(lax.ppermute(block, axis_name, [((i + shift) % n, i) for i in range(n)]))
-    twice = jnp.concatenate(parts + parts, axis=1)
-    start = (n - lax.axis_index(axis_name)) * block.shape[1]
-    return lax.dynamic_slice_in_dim(twice, start, n * block.shape[1], axis=1)
+    index = lax.axis_index(axis_name)
+    width = block.shape[1]
+    full = jnp.zeros((block.shape[0], n * width), block.dtype)
+    for shift in range(n):
+        part = block if shift == 0 else lax.ppermute(block, axis_name, [((i + shift) % n, i) for i in range(n)])
+        full = lax.dynamic_update_slice_in_dim(full, part, ((index + shift) % n) * width, axis=1)
+    return full
 
 
 def product_dot(a, b):
@@ -39,7 +40,7 @@
     keep_half = lax.dynamic_slice_in_dim(ham_vals, layer * half, half, axis=1)
     ham_panel = lax.all_gather(jnp.concatenate([send_half, keep_half], axis=1), "row", axis=0, tiled=True)
     dens_row = gather_cols(dens_vals, "col", n_col)
-    step = half // 2
+    step = half // 4
     received = jnp.concatenate(
         [
             lax.ppermute(product_dot(dens_row, ham_panel[:, i:i + step]), "layer", [(0, 1), (1, 0)])

time: 327 us -> 321 us (0.982)
  waiting for transfers between devices: 239 us -> 225 us
  starting transfers between devices: 12.1 us -> 18.7 us
    unnamed x27 -> x13, local copies, waits for them, and re-layouts: 15.3 us -> 3.59 us
    ppermute x2 -> x4, waiting for transfers between devices: 53.6 us -> 42.9 us  [shards(): lax.ppermute(product_dot(dens_row, ham_panel[:, i:i + step]), 'layer', [(...]
    dynamic_update_slice x0 -> x7, local copies, waits for them, and re-layouts: none -> 10 us  [gather_cols(): lax.dynamic_update_slice_in_dim(full, part, (index + shift) % n * width,...]
    ppermute x7, waiting for transfers between devices: 46.6 us -> 39.5 us  [gather_cols(): lax.ppermute(block, axis_name, [((i + shift) % n, i) for i in range(n)])]
    ppermute x2 -> x4, starting transfers between devices: 5.93 us -> 12.6 us  [shards(): lax.ppermute(product_dot(dens_row, ham_panel[:, i:i + step]), 'layer', [(...]
    all_gather x1, waiting for transfers between devices: 138 us -> 143 us  [shards(): lax.all_gather(jnp.concatenate([send_half, keep_half], axis=1), 'row', ax...]
    dot_general x3 -> x5, matrix products: 38.5 us -> 40.3 us  [product_dot(): jnp.dot(a, b, precision=lax.Precision.HIGH, preferred_element_type=jnp.fl...]
  transfers between devices with their start and end apart: 10 -> 12, of which waited for: 6 -> 8; matrix products, arithmetic and copies ran while one was open for 13% -> 16% of each run, Pallas kernels for 0% -> 0%
where the time goes in v7:
time: 321 us; the launch traced here: 320 us
  waiting for transfers between devices  225 us (70%)
  matrix products  40.3 us (13%)
  starting transfers between devices  18.7 us (6%)
  local copies, waits for them, and re-layouts  17.6 us (5%)
  between operations  13.7 us (4%)
  other arithmetic  4.64 us (1%)
    all_gather x1, waiting for transfers between devices, shards(): lax.all_gather(jnp.concatenate([send_half, keep_half], axis=1), 'row', ax...  143 us
    ppermute x4, waiting for transfers between devices, shards(): lax.ppermute(product_dot(dens_row, ham_panel[:, i:i + step]), 'layer', [(...  42.9 us
    dot_general x5, matrix products, product_dot(): jnp.dot(a, b, precision=lax.Precision.HIGH, preferred_element_type=jnp.fl...  40.3 us
    ppermute x7, waiting for transfers between devices, gather_cols(): lax.ppermute(block, axis_name, [((i + shift) % n, i) for i in range(n)])  39.5 us
    ppermute x4, starting transfers between devices, shards(): lax.ppermute(product_dot(dens_row, ham_panel[:, i:i + step]), 'layer', [(...  12.6 us
    dynamic_update_slice x7, local copies, waits for them, and re-layouts, gather_cols(): lax.dynamic_update_slice_in_dim(full, part, (index + shift) % n * width,...  10 us
  transfers between devices with their start and end apart: 12, of which 8 were waited for; matrix products, arithmetic and copies ran while one was open for 16% of the time, Pallas kernels for 0%

profile of v7, /device:TPU:24, one launch (start us, length us, event | category | flops | bytes accessed | tf_op | source)
XLA Modules:
  0.0 320.0 jit_solution(4222693441157176431)
XLA Ops:
  6.5 0.7 fusion.12
  7.2 0.1 copy.9
  7.3 0.1 broadcast_in_dim.30
  7.4 0.1 reshape.23
  7.5 1.6 copy.8
  9.1 0.1 bitcast_multiply_fusion
  9.2 0.1 constant_dynamic-slice_fusion.2
  9.3 1.1 pad_maximum_fusion
  10.4 0.2 copy.7
  10.6 0.1 broadcast_in_dim.26
  10.7 0.1 broadcast_in_dim.27
  10.7 2.5 broadcast_in_dim.25
  13.2 0.9 constant_dynamic-update-slice_fusion.7
  14.1 2.2 collective-permute-start
  16.3 0.8 collective-permute-start.1
  17.2 0.4 collective-permute-start.2
  17.6 2.7 collective-permute-start.3
  20.3 0.1 copy.10
  20.4 0.1 broadcast_in_dim.32
  20.5 0.1 reshape.25
  20.6 0.5 broadcast_in_dim.33
  21.1 0.2 constant_dynamic-slice_fusion
  21.4 1.8 copy.12
  23.2 5.4 %collective-permute-done = f32[512,256]{0,1:T(8,128)} collective-permute-done((f32[512,256]{0,1:T(8,128)S(1)}, f32[512,256]{0,1:T(8,128)}, u32[]{:S(2)}, u32[]{:S(2)}) %collective-permute-start) | collective-permute-done | bytes 524320 | tf_op jit(solution)/shard_map/ppermute | solution.py:19
  28.5 1.9 constant_dynamic-update-slice_fusion.6
  30.4 31.7 %collective-permute-done.1 = f32[512,256]{0,1:T(8,128)} collective-permute-done((f32[512,256]{0,1:T(8,128)S(1)}, f32[512,256]{0,1:T(8,128)}, u32[]{:S(2)}, u32[]{:S(2)}) %collective-permute-start.1) | collective-permute-done | bytes 524320 | tf_op jit(solution)/shard_map/ppermute | solution.py:19
  62.1 1.9 constant_dynamic-update-slice_fusion.5
  64.0 1.9 constant_dynamic-update-slice_fusion.4
  65.9 1.9 constant_dynamic-update-slice_fusion.3
  67.8 0.8 constant_dynamic-update-slice_fusion.2
  68.6 0.8 constant_dynamic-update-slice_fusion.1
  69.5 2.5 collective-permute-done.6
  71.9 0.8 constant_dynamic-update-slice_fusion
  72.8 142.6 %all-gather.2.cloned.1.call-done = f32[2048,2048]{0,1:T(8,128)} async-done(((f32[128,2048]{0,1:T(8,128)}), f32[2048,2048]{0,1:T(8,128)}) %all-gather.2.cloned.1.call-update) | async-done | bytes 16777232 | tf_op jit(solution)/shard_map/all_gather | solution.py:41
  215.4 6.4 %fusion.8 = f32[512,256]{1,0:T(8,128)S(1)} fusion(f32[512,2048]{0,1:T(8,128)} %constant_dynamic-update-slice_fusion, f32[2048,2048]{0,1:T(8,128)} %all-gather.2.cloned.1.call-done), kind=kOutput, calls=%fused_computation.8 | convolution fusion | flops 1610612736 | bytes 6815744 | tf_op jit(solution)/shard_map/dot_general | solution.py:25
  221.8 3.6 %collective-permute-start.7 = (f32[512,256]{1,0:T(8,128)S(1)}, f32[512,256]{1,0:T(8,128)S(1)}, u32[]{:S(2)}, u32[]{:S(2)}) collective-permute-start(f32[512,256]{1,0:T(8,128)S(1)} %fusion.8), channel_id=1, source_target_pairs={{0,1},{1,0},{2,3},{3,2},{4,5},{5,4},{6,7},{7,6},{8,9},{9,8},{10,11... | collective-permute-start | bytes 1572872 | tf_op jit(solution)/shard_map/ppermute | solution.py:46
  225.4 6.3 %fusion.6 = f32[512,256]{1,0:T(8,128)S(1)} fusion(f32[512,2048]{0,1:T(8,128)} %constant_dynamic-update-slice_fusion, f32[2048,2048]{0,1:T(8,128)} %all-gather.2.cloned.1.call-done), kind=kOutput, calls=%fused_computation.6 | convolution fusion | flops 1610612736 | bytes 6815744 | tf_op jit(solution)/shard_map/dot_general | solution.py:25
  231.7 2.7 collective-permute-start.8
  234.4 6.3 %fusion.4 = f32[512,256]{1,0:T(8,128)S(1)} fusion(f32[512,2048]{0,1:T(8,128)} %constant_dynamic-update-slice_fusion, f32[2048,2048]{0,1:T(8,128)} %all-gather.2.cloned.1.call-done), kind=kOutput, calls=%fused_computation.4 | convolution fusion | flops 1610612736 | bytes 6815744 | tf_op jit(solution)/shard_map/dot_general | solution.py:25
  240.7 3.4 %collective-permute-start.9 = (f32[512,256]{1,0:T(8,128)S(1)}, f32[512,256]{1,0:T(8,128)S(1)}, u32[]{:S(2)}, u32[]{:S(2)}) collective-permute-start(f32[512,256]{1,0:T(8,128)S(1)} %fusion.4), channel_id=1, source_target_pairs={{0,1},{1,0},{2,3},{3,2},{4,5},{5,4},{6,7},{7,6},{8,9},{9,8},{10,11... | collective-permute-start | bytes 1572872 | tf_op jit(solution)/shard_map/ppermute | solution.py:46
  244.1 5.7 %fusion.2 = f32[512,256]{1,0:T(8,128)S(1)} fusion(f32[512,2048]{0,1:T(8,128)} %constant_dynamic-update-slice_fusion, f32[2048,2048]{0,1:T(8,128)S(1)} %copy-done.1), kind=kOutput, calls=%fused_computation.2 | convolution fusion | flops 1610612736 | bytes 6815744 | tf_op jit(solution)/shard_map/dot_general | solution.py:25
  249.8 2.9 collective-permute-start.10
  252.7 15.6 %fusion = f32[512,1024]{1,0:T(8,128)S(1)} fusion(f32[512,2048]{0,1:T(8,128)} %constant_dynamic-update-slice_fusion, f32[2048,2048]{0,1:T(8,128)S(1)} %copy-done.1), kind=kOutput, calls=%fused_computation | convolution fusion | flops 6442450944 | bytes 14680064 | tf_op jit(solution)/shard_map/dot_general | solution.py:25
  268.4 13.4 %collective-permute-done.7 = f32[512,256]{1,0:T(8,128)S(1)} collective-permute-done((f32[512,256]{1,0:T(8,128)S(1)}, f32[512,256]{1,0:T(8,128)S(1)}, u32[]{:S(2)}, u32[]{:S(2)}) %collective-permute-start.7) | collective-permute-done | bytes 524320 | tf_op jit(solution)/shard_map/ppermute | solution.py:46
  281.7 12.7 %collective-permute-done.8 = f32[512,256]{1,0:T(8,128)S(1)} collective-permute-done((f32[512,256]{1,0:T(8,128)S(1)}, f32[512,256]{1,0:T(8,128)S(1)}, u32[]{:S(2)}, u32[]{:S(2)}) %collective-permute-start.8) | collective-permute-done | bytes 524320 | tf_op jit(solution)/shard_map/ppermute | solution.py:46
  294.4 11.2 %collective-permute-done.9 = f32[512,256]{1,0:T(8,128)S(1)} collective-permute-done((f32[512,256]{1,0:T(8,128)S(1)}, f32[512,256]{1,0:T(8,128)S(1)}, u32[]{:S(2)}, u32[]{:S(2)}) %collective-permute-start.9) | collective-permute-done | bytes 524320 | tf_op jit(solution)/shard_map/ppermute | solution.py:46
  305.6 5.6 %collective-permute-done.10 = f32[512,256]{1,0:T(8,128)S(1)} collective-permute-done((f32[512,256]{1,0:T(8,128)S(1)}, f32[512,256]{1,0:T(8,128)S(1)}, u32[]{:S(2)}, u32[]{:S(2)}) %collective-permute-start.10) | collective-permute-done | bytes 524320 | tf_op jit(solution)/shard_map/ppermute | solution.py:46
  311.3 1.9 fusion.10
  (21 shorter events, 0.1 us)
Async XLA Ops:
  6.5 208.8 %all-gather.2.cloned.1.call-start = ((), (), s32[]{:S(2)}) async-start(), calls=%async_computation | async-start | bytes 17825792 | tf_op jit(solution)/shard_map/all_gather | solution.py:41
  9.1 1.3 copy-start.2
  9.1 1.5 copy-start.4
  10.3 10.0 %copy-start.3 = (s32[8,32]{1,0:T(8,128)S(1)}, s32[8,32]{1,0:T(8,128)}, u32[]{:S(2)}) copy-start(s32[8,32]{1,0:T(8,128)} %param.9) | copy-start | bytes 3076
  14.1 14.4 %collective-permute-start = (f32[512,256]{0,1:T(8,128)S(1)}, f32[512,256]{0,1:T(8,128)}, u32[]{:S(2)}, u32[]{:S(2)}) collective-permute-start(f32[512,256]{0,1:T(8,128)S(1)} %bitcast.25), channel_id=1, source_target_pairs={{2,0},{4,2},{6,4},{8,6},{10,8},{12,10},{14,12},{0,14},{3,1},{5,3},... | collective-permute-start | bytes 1572872 | tf_op jit(solution)/shard_map/ppermute | solution.py:19
  16.3 45.8 %collective-permute-start.1 = (f32[512,256]{0,1:T(8,128)S(1)}, f32[512,256]{0,1:T(8,128)}, u32[]{:S(2)}, u32[]{:S(2)}) collective-permute-start(f32[512,256]{0,1:T(8,128)S(1)} %bitcast.26), channel_id=1, source_target_pairs={{4,0},{6,2},{8,4},{10,6},{12,8},{14,10},{0,12},{2,14},{5,1},{7,3},... | collective-permute-start | bytes 1572872 | tf_op jit(solution)/shard_map/ppermute | solution.py:19
  17.2 46.8 %collective-permute-start.2 = (f32[512,256]{0,1:T(8,128)S(1)}, f32[512,256]{0,1:T(8,128)}, u32[]{:S(2)}, u32[]{:S(2)}) collective-permute-start(f32[512,256]{0,1:T(8,128)S(1)} %bitcast.27), channel_id=1, source_target_pairs={{6,0},{8,2},{10,4},{12,6},{14,8},{0,10},{2,12},{4,14},{7,1},{9,3},... | collective-permute-start | bytes 1572872 | tf_op jit(solution)/shard_map/ppermute | solution.py:19
  17.6 48.3 %collective-permute-start.3 = (f32[512,256]{0,1:T(8,128)S(1)}, f32[512,256]{0,1:T(8,128)}, u32[]{:S(2)}, u32[]{:S(2)}) collective-permute-start(f32[512,256]{0,1:T(8,128)S(1)} %bitcast.28), channel_id=1, source_target_pairs={{8,0},{10,2},{12,4},{14,6},{0,8},{2,10},{4,12},{6,14},{9,1},{11,3}... | collective-permute-start | bytes 1572872 | tf_op jit(solution)/shard_map/ppermute | solution.py:19
  20.3 47.5 %collective-permute-start.4 = (f32[512,256]{0,1:T(8,128)S(1)}, f32[512,256]{0,1:T(8,128)S(1)}, u32[]{:S(2)}, u32[]{:S(2)}) collective-permute-start(f32[512,256]{0,1:T(8,128)S(1)} %bitcast.29), channel_id=1, source_target_pairs={{10,0},{12,2},{14,4},{0,6},{2,8},{4,10},{6,12},{8,14},{11,1},{13,3... | collective-permute-start | bytes 1572872 | tf_op jit(solution)/shard_map/ppermute | solution.py:19
  28.5 40.1 %collective-permute-start.5 = (f32[512,256]{0,1:T(8,128)S(1)}, f32[512,256]{0,1:T(8,128)S(1)}, u32[]{:S(2)}, u32[]{:S(2)}) collective-permute-start(f32[512,256]{0,1:T(8,128)S(1)} %bitcast.30), channel_id=1, source_target_pairs={{12,0},{14,2},{0,4},{2,6},{4,8},{6,10},{8,12},{10,14},{13,1},{15,3... | collective-permute-start | bytes 1572872 | tf_op jit(solution)/shard_map/ppermute | solution.py:19
  62.1 9.8 %collective-permute-start.6 = (f32[512,256]{0,1:T(8,128)S(1)}, f32[512,256]{0,1:T(8,128)S(1)}, u32[]{:S(2)}, u32[]{:S(2)}) collective-permute-start(f32[512,256]{0,1:T(8,128)S(1)} %bitcast.31), channel_id=1, source_target_pairs={{14,0},{0,2},{2,4},{4,6},{6,8},{8,10},{10,12},{12,14},{15,1},{1,3}... | collective-permute-start | bytes 1572872 | tf_op jit(solution)/shard_map/ppermute | solution.py:19
  215.4 28.7 %copy-start.1 = (f32[2048,2048]{0,1:T(8,128)S(1)}, f32[2048,2048]{0,1:T(8,128)}, u32[]{:S(2)}) copy-start(f32[2048,2048]{0,1:T(8,128)} %all-gather.2.cloned.1.call-done) | copy-start | bytes 50331652
  221.8 59.9 %collective-permute-start.7 = (f32[512,256]{1,0:T(8,128)S(1)}, f32[512,256]{1,0:T(8,128)S(1)}, u32[]{:S(2)}, u32[]{:S(2)}) collective-permute-start(f32[512,256]{1,0:T(8,128)S(1)} %fusion.8), channel_id=1, source_target_pairs={{0,1},{1,0},{2,3},{3,2},{4,5},{5,4},{6,7},{7,6},{8,9},{9,8},{10,11... | collective-permute-start | bytes 1572872 | tf_op jit(solution)/shard_map/ppermute | solution.py:46
  231.7 62.7 %collective-permute-start.8 = (f32[512,256]{1,0:T(8,128)S(1)}, f32[512,256]{1,0:T(8,128)S(1)}, u32[]{:S(2)}, u32[]{:S(2)}) collective-permute-start(f32[512,256]{1,0:T(8,128)S(1)} %fusion.6), channel_id=1, source_target_pairs={{0,1},{1,0},{2,3},{3,2},{4,5},{5,4},{6,7},{7,6},{8,9},{9,8},{10,11... | collective-permute-start | bytes 1572872 | tf_op jit(solution)/shard_map/ppermute | solution.py:46
  240.7 64.9 %collective-permute-start.9 = (f32[512,256]{1,0:T(8,128)S(1)}, f32[512,256]{1,0:T(8,128)S(1)}, u32[]{:S(2)}, u32[]{:S(2)}) collective-permute-start(f32[512,256]{1,0:T(8,128)S(1)} %fusion.4), channel_id=1, source_target_pairs={{0,1},{1,0},{2,3},{3,2},{4,5},{5,4},{6,7},{7,6},{8,9},{9,8},{10,11... | collective-permute-start | bytes 1572872 | tf_op jit(solution)/shard_map/ppermute | solution.py:46
  249.8 61.5 %copy-start = (f32[512,1024]{1,0:T(8,128)S(1)}, f32[512,1024]{1,0:T(8,128)}, u32[]{:S(2)}) copy-start(f32[512,1024]{1,0:T(8,128)} %copy.12) | copy-start | bytes 6291460
  249.8 61.4 %collective-permute-start.10 = (f32[512,256]{1,0:T(8,128)S(1)}, f32[512,256]{1,0:T(8,128)S(1)}, u32[]{:S(2)}, u32[]{:S(2)}) collective-permute-start(f32[512,256]{1,0:T(8,128)S(1)} %fusion.2), channel_id=1, source_target_pairs={{0,1},{1,0},{2,3},{3,2},{4,5},{5,4},{6,7},{7,6},{8,9},{9,8},{10,11... | collective-permute-start | bytes 1572872 | tf_op jit(solution)/shard_map/ppermute | solution.py:46
Sparse Core Ops, SparseCore 0:
  10.5 204.8 all-gather.1

commit v8 on v7

--- a/solution.py
+++ b/solution.py
@@ -36,19 +36,24 @@
     half = ham_vals.shape[1] // 2
     kept = lax.dynamic_slice_in_dim(expand(filter_mask), layer * half, half, axis=1)
 
-    send_half = lax.dynamic_slice_in_dim(ham_vals, (1 - layer) * half, half, axis=1)
-    keep_half = lax.dynamic_slice_in_dim(ham_vals, layer * half, half, axis=1)
-    ham_panel = lax.all_gather(jnp.concatenate([send_half, keep_half], axis=1), "row", axis=0, tiled=True)
+    ham_panel = lax.all_gather(ham_vals, "row", axis=0, tiled=True)
     dens_row = gather_cols(dens_vals, "col", n_col)
     step = half // 4
+    send_start = (1 - layer) * half
     received = jnp.concatenate(
         [
-            lax.ppermute(product_dot(dens_row, ham_panel[:, i:i + step]), "layer", [(0, 1), (1, 0)])
+            lax.ppermute(
+                product_dot(dens_row, lax.dynamic_slice_in_dim(ham_panel, send_start + i, step, axis=1)),
+                "layer",
+                [(0, 1), (1, 0)],
+            )
             for i in range(0, half, step)
         ],
         axis=1,
     )
-    own = lax.optimization_barrier(product_dot(dens_row, ham_panel[:, half:]))
+    own = lax.optimization_barrier(
+        product_dot(dens_row, lax.dynamic_slice_in_dim(ham_panel, layer * half, half, axis=1))
+    )
     return (own + received) * kept
 
 

time: 321 us -> 321 us (level)
  no operation moved by 1% of the time
where the time goes in v8:
time: 321 us; the launch traced here: 320 us
  waiting for transfers between devices  225 us (70%)
  matrix products  40.4 us (13%)
  starting transfers between devices  18.7 us (6%)
  local copies, waits for them, and re-layouts  17.5 us (5%)
  between operations  13.6 us (4%)
  other arithmetic  4.62 us (1%)
    all_gather x1, waiting for transfers between devices, shards(): ham_panel = lax.all_gather(ham_vals, 'row', axis=0, tiled=True)  143 us
    ppermute x4, waiting for transfers between devices, shards(): lax.ppermute(product_dot(dens_row, lax.dynamic_slice_in_dim(ham_panel, se...  42.9 us
    dot_general x5, matrix products, product_dot(): jnp.dot(a, b, precision=lax.Precision.HIGH, preferred_element_type=jnp.fl...  40.4 us
    ppermute x7, waiting for transfers between devices, gather_cols(): lax.ppermute(block, axis_name, [((i + shift) % n, i) for i in range(n)])  39.5 us
    ppermute x4, starting transfers between devices, shards(): lax.ppermute(product_dot(dens_row, lax.dynamic_slice_in_dim(ham_panel, se...  12.6 us
    dynamic_update_slice x7, local copies, waits for them, and re-layouts, gather_cols(): lax.dynamic_update_slice_in_dim(full, part, (index + shift) % n * width,...  10 us
  transfers between devices with their start and end apart: 12, of which 8 were waited for; matrix products, arithmetic and copies ran while one was open for 16% of the time, Pallas kernels for 0%

profile of v8, /device:TPU:24, one launch (start us, length us, event | category | flops | bytes accessed | tf_op | source)
XLA Modules:
  0.0 320.0 jit_solution(16905548273761662166)
XLA Ops:
  6.5 0.8 fusion.17
  7.3 0.1 copy.9
  7.4 0.1 broadcast_in_dim.30
  7.5 0.1 reshape.23
  7.6 1.6 copy.8
  9.1 1.0 bitcast_multiply_fusion
  10.2 0.0 all-gather.2.cloned.1.call-update
  10.2 0.2 copy.7
  10.5 0.1 broadcast_in_dim.26
  10.5 0.1 broadcast_in_dim.27
  10.6 2.5 broadcast_in_dim.25
  13.1 0.9 constant_dynamic-update-slice_fusion.7
  14.0 2.2 collective-permute-start
  16.2 0.8 collective-permute-start.1
  17.0 0.4 collective-permute-start.2
  17.4 2.7 collective-permute-start.3
  20.1 0.1 copy.10
  20.2 0.1 broadcast_in_dim.32
  20.3 0.1 reshape.25
  20.4 0.5 broadcast_in_dim.33
  20.9 0.2 constant_dynamic-slice_fusion
  21.2 1.8 copy.12
  23.0 5.4 %collective-permute-done = f32[512,256]{0,1:T(8,128)} collective-permute-done((f32[512,256]{0,1:T(8,128)S(1)}, f32[512,256]{0,1:T(8,128)}, u32[]{:S(2)}, u32[]{:S(2)}) %collective-permute-start) | collective-permute-done | bytes 524320 | tf_op jit(solution)/shard_map/ppermute | solution.py:19
  28.4 1.9 constant_dynamic-update-slice_fusion.6
  30.3 31.7 %collective-permute-done.1 = f32[512,256]{0,1:T(8,128)} collective-permute-done((f32[512,256]{0,1:T(8,128)S(1)}, f32[512,256]{0,1:T(8,128)}, u32[]{:S(2)}, u32[]{:S(2)}) %collective-permute-start.1) | collective-permute-done | bytes 524320 | tf_op jit(solution)/shard_map/ppermute | solution.py:19
  62.0 1.9 constant_dynamic-update-slice_fusion.5
  63.9 1.9 constant_dynamic-update-slice_fusion.4
  65.8 1.9 constant_dynamic-update-slice_fusion.3
  67.7 0.8 constant_dynamic-update-slice_fusion.2
  68.5 0.8 constant_dynamic-update-slice_fusion.1
  69.3 2.5 collective-permute-done.6
  71.8 0.8 constant_dynamic-update-slice_fusion
  72.6 142.6 %all-gather.2.cloned.1.call-done = f32[2048,2048]{0,1:T(8,128)} async-done(((f32[128,2048]{0,1:T(8,128)}), f32[2048,2048]{0,1:T(8,128)}) %all-gather.2.cloned.1.call-update) | async-done | bytes 16777232 | tf_op jit(solution)/shard_map/all_gather | solution.py:39
  215.2 6.4 %fusion.3 = f32[512,256]{1,0:T(8,128)S(1)} fusion(f32[512,2048]{0,1:T(8,128)} %constant_dynamic-update-slice_fusion, f32[2048,2048]{0,1:T(8,128)} %all-gather.2.cloned.1.call-done, s32[]{:T(128)S(6)} %select_n.99), kind=kOutput, calls=%fused_computation.4 | convolution fusion | flops 1610612736 | bytes 6815748 | tf_op jit(solution)/shard_map/dot_general | solution.py:25
  221.7 3.4 %collective-permute-start.10 = (f32[512,256]{1,0:T(8,128)S(1)}, f32[512,256]{1,0:T(8,128)S(1)}, u32[]{:S(2)}, u32[]{:S(2)}) collective-permute-start(f32[512,256]{1,0:T(8,128)S(1)} %fusion.3), channel_id=1, source_target_pairs={{0,1},{1,0},{2,3},{3,2},{4,5},{5,4},{6,7},{7,6},{8,9},{9,8},{10,11... | collective-permute-start | bytes 1572872 | tf_op jit(solution)/shard_map/ppermute | solution.py:45
  225.1 6.3 %fusion.7 = f32[512,256]{1,0:T(8,128)S(1)} fusion(f32[512,2048]{0,1:T(8,128)} %constant_dynamic-update-slice_fusion, f32[2048,2048]{0,1:T(8,128)} %all-gather.2.cloned.1.call-done, s32[]{:T(128)S(6)} %select_n.97), kind=kOutput, calls=%fused_computation.8 | convolution fusion | flops 1610612736 | bytes 6815748 | tf_op jit(solution)/shard_map/dot_general | solution.py:25
  231.4 2.9 collective-permute-start.8
  234.3 6.3 %fusion.5 = f32[512,256]{1,0:T(8,128)S(1)} fusion(f32[512,2048]{0,1:T(8,128)} %constant_dynamic-update-slice_fusion, f32[2048,2048]{0,1:T(8,128)} %all-gather.2.cloned.1.call-done, s32[]{:T(128)S(6)} %select_n.98), kind=kOutput, calls=%fused_computation.6 | convolution fusion | flops 1610612736 | bytes 6815748 | tf_op jit(solution)/shard_map/dot_general | solution.py:25
  240.6 3.3 %collective-permute-start.9 = (f32[512,256]{1,0:T(8,128)S(1)}, f32[512,256]{1,0:T(8,128)S(1)}, u32[]{:S(2)}, u32[]{:S(2)}) collective-permute-start(f32[512,256]{1,0:T(8,128)S(1)} %fusion.5), channel_id=1, source_target_pairs={{0,1},{1,0},{2,3},{3,2},{4,5},{5,4},{6,7},{7,6},{8,9},{9,8},{10,11... | collective-permute-start | bytes 1572872 | tf_op jit(solution)/shard_map/ppermute | solution.py:45
  243.8 5.7 %fusion.9 = f32[512,256]{1,0:T(8,128)S(1)} fusion(f32[512,2048]{0,1:T(8,128)} %constant_dynamic-update-slice_fusion, f32[2048,2048]{0,1:T(8,128)S(1)} %copy-done.1, s32[]{:T(128)S(6)} %select_n.96), kind=kOutput, calls=%fused_computation.10 | convolution fusion | flops 1610612736 | bytes 6815748 | tf_op jit(solution)/shard_map/dot_general | solution.py:25
  249.5 0.0 copy-start
  249.5 3.1 collective-permute-start.7
  252.6 15.8 %fusion = f32[512,1024]{1,0:T(8,128)S(1)} fusion(f32[512,2048]{0,1:T(8,128)} %constant_dynamic-update-slice_fusion, f32[2048,2048]{0,1:T(8,128)S(1)} %copy-done.1, s32[]{:T(128)S(6)} %select_n.95), kind=kOutput, calls=%fused_computation | convolution fusion | flops 6442450944 | bytes 14680068 | tf_op jit(solution)/shard_map/dot_general | solution.py:25
  268.4 8.1 %collective-permute-done.10 = f32[512,256]{1,0:T(8,128)S(1)} collective-permute-done((f32[512,256]{1,0:T(8,128)S(1)}, f32[512,256]{1,0:T(8,128)S(1)}, u32[]{:S(2)}, u32[]{:S(2)}) %collective-permute-start.10) | collective-permute-done | bytes 524320 | tf_op jit(solution)/shard_map/ppermute | solution.py:45
  276.5 18.0 %collective-permute-done.8 = f32[512,256]{1,0:T(8,128)S(1)} collective-permute-done((f32[512,256]{1,0:T(8,128)S(1)}, f32[512,256]{1,0:T(8,128)S(1)}, u32[]{:S(2)}, u32[]{:S(2)}) %collective-permute-start.8) | collective-permute-done | bytes 524320 | tf_op jit(solution)/shard_map/ppermute | solution.py:45
  294.5 11.2 %collective-permute-done.9 = f32[512,256]{1,0:T(8,128)S(1)} collective-permute-done((f32[512,256]{1,0:T(8,128)S(1)}, f32[512,256]{1,0:T(8,128)S(1)}, u32[]{:S(2)}, u32[]{:S(2)}) %collective-permute-start.9) | collective-permute-done | bytes 524320 | tf_op jit(solution)/shard_map/ppermute | solution.py:45
  305.6 5.6 %collective-permute-done.7 = f32[512,256]{1,0:T(8,128)S(1)} collective-permute-done((f32[512,256]{1,0:T(8,128)S(1)}, f32[512,256]{1,0:T(8,128)S(1)}, u32[]{:S(2)}, u32[]{:S(2)}) %collective-permute-start.7) | collective-permute-done | bytes 524320 | tf_op jit(solution)/shard_map/ppermute | solution.py:45
  311.2 1.9 fusion.2
  (19 shorter events, 0.0 us)
Async XLA Ops:
  6.5 3.7 %copy-start.2 = (f32[1,512,256]{2,1,0:T(8,128)S(1)}, f32[1,512,256]{2,1,0:T(8,128)}, u32[]{:S(2)}) copy-start(f32[1,512,256]{2,1,0:T(8,128)} %param.5) | copy-start | bytes 1572868
  6.5 3.9 %copy-start.4 = (s32[1,8,4]{1,2,0:T(4,128)S(1)}, s32[1,8,4]{1,2,0:T(4,128)}, u32[]{:S(2)}) copy-start(s32[1,8,4]{1,2,0:T(4,128)} %param.6) | copy-start | bytes 388
  6.5 208.7 %all-gather.2.cloned.1.call-start = ((), (), s32[]{:S(2)}) async-start(), calls=%async_computation | async-start | bytes 17825792 | tf_op jit(solution)/shard_map/all_gather | solution.py:39
  10.2 10.0 %copy-start.3 = (s32[8,32]{1,0:T(8,128)S(1)}, s32[8,32]{1,0:T(8,128)}, u32[]{:S(2)}) copy-start(s32[8,32]{1,0:T(8,128)} %param.9) | copy-start | bytes 3076
  14.0 14.4 %collective-permute-start = (f32[512,256]{0,1:T(8,128)S(1)}, f32[512,256]{0,1:T(8,128)}, u32[]{:S(2)}, u32[]{:S(2)}) collective-permute-start(f32[512,256]{0,1:T(8,128)S(1)} %bitcast.25), channel_id=1, source_target_pairs={{2,0},{4,2},{6,4},{8,6},{10,8},{12,10},{14,12},{0,14},{3,1},{5,3},... | collective-permute-start | bytes 1572872 | tf_op jit(solution)/shard_map/ppermute | solution.py:19
  16.2 45.8 %collective-permute-start.1 = (f32[512,256]{0,1:T(8,128)S(1)}, f32[512,256]{0,1:T(8,128)}, u32[]{:S(2)}, u32[]{:S(2)}) collective-permute-start(f32[512,256]{0,1:T(8,128)S(1)} %bitcast.26), channel_id=1, source_target_pairs={{4,0},{6,2},{8,4},{10,6},{12,8},{14,10},{0,12},{2,14},{5,1},{7,3},... | collective-permute-start | bytes 1572872 | tf_op jit(solution)/shard_map/ppermute | solution.py:19
  17.0 46.8 %collective-permute-start.2 = (f32[512,256]{0,1:T(8,128)S(1)}, f32[512,256]{0,1:T(8,128)}, u32[]{:S(2)}, u32[]{:S(2)}) collective-permute-start(f32[512,256]{0,1:T(8,128)S(1)} %bitcast.27), channel_id=1, source_target_pairs={{6,0},{8,2},{10,4},{12,6},{14,8},{0,10},{2,12},{4,14},{7,1},{9,3},... | collective-permute-start | bytes 1572872 | tf_op jit(solution)/shard_map/ppermute | solution.py:19
  17.4 48.4 %collective-permute-start.3 = (f32[512,256]{0,1:T(8,128)S(1)}, f32[512,256]{0,1:T(8,128)}, u32[]{:S(2)}, u32[]{:S(2)}) collective-permute-start(f32[512,256]{0,1:T(8,128)S(1)} %bitcast.28), channel_id=1, source_target_pairs={{8,0},{10,2},{12,4},{14,6},{0,8},{2,10},{4,12},{6,14},{9,1},{11,3}... | collective-permute-start | bytes 1572872 | tf_op jit(solution)/shard_map/ppermute | solution.py:19
  20.1 47.5 %collective-permute-start.4 = (f32[512,256]{0,1:T(8,128)S(1)}, f32[512,256]{0,1:T(8,128)S(1)}, u32[]{:S(2)}, u32[]{:S(2)}) collective-permute-start(f32[512,256]{0,1:T(8,128)S(1)} %bitcast.29), channel_id=1, source_target_pairs={{10,0},{12,2},{14,4},{0,6},{2,8},{4,10},{6,12},{8,14},{11,1},{13,3... | collective-permute-start | bytes 1572872 | tf_op jit(solution)/shard_map/ppermute | solution.py:19
  28.4 40.1 %collective-permute-start.5 = (f32[512,256]{0,1:T(8,128)S(1)}, f32[512,256]{0,1:T(8,128)S(1)}, u32[]{:S(2)}, u32[]{:S(2)}) collective-permute-start(f32[512,256]{0,1:T(8,128)S(1)} %bitcast.30), channel_id=1, source_target_pairs={{12,0},{14,2},{0,4},{2,6},{4,8},{6,10},{8,12},{10,14},{13,1},{15,3... | collective-permute-start | bytes 1572872 | tf_op jit(solution)/shard_map/ppermute | solution.py:19
  62.0 9.8 %collective-permute-start.6 = (f32[512,256]{0,1:T(8,128)S(1)}, f32[512,256]{0,1:T(8,128)S(1)}, u32[]{:S(2)}, u32[]{:S(2)}) collective-permute-start(f32[512,256]{0,1:T(8,128)S(1)} %bitcast.31), channel_id=1, source_target_pairs={{14,0},{0,2},{2,4},{4,6},{6,8},{8,10},{10,12},{12,14},{15,1},{1,3}... | collective-permute-start | bytes 1572872 | tf_op jit(solution)/shard_map/ppermute | solution.py:19
  215.2 28.6 %copy-start.1 = (f32[2048,2048]{0,1:T(8,128)S(1)}, f32[2048,2048]{0,1:T(8,128)}, u32[]{:S(2)}) copy-start(f32[2048,2048]{0,1:T(8,128)} %all-gather.2.cloned.1.call-done) | copy-start | bytes 50331652
  221.7 54.8 %collective-permute-start.10 = (f32[512,256]{1,0:T(8,128)S(1)}, f32[512,256]{1,0:T(8,128)S(1)}, u32[]{:S(2)}, u32[]{:S(2)}) collective-permute-start(f32[512,256]{1,0:T(8,128)S(1)} %fusion.3), channel_id=1, source_target_pairs={{0,1},{1,0},{2,3},{3,2},{4,5},{5,4},{6,7},{7,6},{8,9},{9,8},{10,11... | collective-permute-start | bytes 1572872 | tf_op jit(solution)/shard_map/ppermute | solution.py:45
  231.4 63.0 %collective-permute-start.8 = (f32[512,256]{1,0:T(8,128)S(1)}, f32[512,256]{1,0:T(8,128)S(1)}, u32[]{:S(2)}, u32[]{:S(2)}) collective-permute-start(f32[512,256]{1,0:T(8,128)S(1)} %fusion.7), channel_id=1, source_target_pairs={{0,1},{1,0},{2,3},{3,2},{4,5},{5,4},{6,7},{7,6},{8,9},{9,8},{10,11... | collective-permute-start | bytes 1572872 | tf_op jit(solution)/shard_map/ppermute | solution.py:45
  240.6 65.0 %collective-permute-start.9 = (f32[512,256]{1,0:T(8,128)S(1)}, f32[512,256]{1,0:T(8,128)S(1)}, u32[]{:S(2)}, u32[]{:S(2)}) collective-permute-start(f32[512,256]{1,0:T(8,128)S(1)} %fusion.5), channel_id=1, source_target_pairs={{0,1},{1,0},{2,3},{3,2},{4,5},{5,4},{6,7},{7,6},{8,9},{9,8},{10,11... | collective-permute-start | bytes 1572872 | tf_op jit(solution)/shard_map/ppermute | solution.py:45
  249.5 61.7 %copy-start = (f32[512,1024]{1,0:T(8,128)S(1)}, f32[512,1024]{1,0:T(8,128)}, u32[]{:S(2)}) copy-start(f32[512,1024]{1,0:T(8,128)} %copy.12) | copy-start | bytes 6291460
  249.5 61.7 %collective-permute-start.7 = (f32[512,256]{1,0:T(8,128)S(1)}, f32[512,256]{1,0:T(8,128)S(1)}, u32[]{:S(2)}, u32[]{:S(2)}) collective-permute-start(f32[512,256]{1,0:T(8,128)S(1)} %fusion.9), channel_id=1, source_target_pairs={{0,1},{1,0},{2,3},{3,2},{4,5},{5,4},{6,7},{7,6},{8,9},{9,8},{10,11... | collective-permute-start | bytes 1572872 | tf_op jit(solution)/shard_map/ppermute | solution.py:45
Sparse Core Ops, SparseCore 0:
  10.3 204.8 all-gather.1

commit v9 on v7

--- a/solution.py
+++ b/solution.py
@@ -40,11 +40,11 @@
     keep_half = lax.dynamic_slice_in_dim(ham_vals, layer * half, half, axis=1)
     ham_panel = lax.all_gather(jnp.concatenate([send_half, keep_half], axis=1), "row", axis=0, tiled=True)
     dens_row = gather_cols(dens_vals, "col", n_col)
-    step = half // 4
+    bounds = [0, half // 4, half // 2, half]
     received = jnp.concatenate(
         [
-            lax.ppermute(product_dot(dens_row, ham_panel[:, i:i + step]), "layer", [(0, 1), (1, 0)])
-            for i in range(0, half, step)
+            lax.ppermute(product_dot(dens_row, ham_panel[:, a:b]), "layer", [(0, 1), (1, 0)])
+            for a, b in zip(bounds[:-1], bounds[1:])
         ],
         axis=1,
     )

time: 321 us -> 322 us (level)
  waiting for transfers between devices: 225 us -> 230 us
    ppermute x4 -> x3, waiting for transfers between devices: 42.9 us -> 47.9 us  [shards(): lax.ppermute(product_dot(dens_row, ham_panel[:, a:b]), 'layer', [(0, 1),...]
    ppermute x4 -> x3, starting transfers between devices: 12.6 us -> 9.58 us  [shards(): lax.ppermute(product_dot(dens_row, ham_panel[:, a:b]), 'layer', [(0, 1),...]
    dot_general x5 -> x4, matrix products: 40.3 us -> 38.4 us  [product_dot(): jnp.dot(a, b, precision=lax.Precision.HIGH, preferred_element_type=jnp.fl...]
  transfers between devices with their start and end apart: 12 -> 11, of which waited for: 8 -> 6; matrix products, arithmetic and copies ran while one was open for 16% -> 15% of each run, Pallas kernels for 0% -> 0%
where the time goes in v9:
time: 322 us; the launch traced here: 320 us
  waiting for transfers between devices  230 us (71%)
  matrix products  38.4 us (12%)
  local copies, waits for them, and re-layouts  17.6 us (5%)
  starting transfers between devices  15.7 us (5%)
  between operations  13.7 us (4%)
  other arithmetic  4.68 us (1%)
    all_gather x1, waiting for transfers between devices, shards(): lax.all_gather(jnp.concatenate([send_half, keep_half], axis=1), 'row', ax...  143 us
    ppermute x3, waiting for transfers between devices, shards(): lax.ppermute(product_dot(dens_row, ham_panel[:, a:b]), 'layer', [(0, 1),...  47.9 us
    ppermute x7, waiting for transfers between devices, gather_cols(): lax.ppermute(block, axis_name, [((i + shift) % n, i) for i in range(n)])  39.5 us
    dot_general x4, matrix products, product_dot(): jnp.dot(a, b, precision=lax.Precision.HIGH, preferred_element_type=jnp.fl...  38.4 us
    dynamic_update_slice x7, local copies, waits for them, and re-layouts, gather_cols(): lax.dynamic_update_slice_in_dim(full, part, (index + shift) % n * width,...  10 us
    ppermute x3, starting transfers between devices, shards(): lax.ppermute(product_dot(dens_row, ham_panel[:, a:b]), 'layer', [(0, 1),...  9.58 us
  transfers between devices with their start and end apart: 11, of which 6 were waited for; matrix products, arithmetic and copies ran while one was open for 15% of the time, Pallas kernels for 0%

profile of v9, /device:TPU:24, one launch (start us, length us, event | category | flops | bytes accessed | tf_op | source)
XLA Modules:
  0.0 320.1 jit_solution(5869538176357597726)
XLA Ops:
  6.5 0.7 fusion.10
  7.2 0.1 copy.9
  7.3 0.1 broadcast_in_dim.30
  7.4 0.1 reshape.23
  7.5 1.6 copy.8
  9.1 0.0 copy-start.2
  9.1 0.0 copy-start.4
  9.1 0.1 bitcast_multiply_fusion
  9.2 0.1 constant_dynamic-slice_fusion.2
  9.3 1.0 pad_maximum_fusion
  10.3 0.0 all-gather.2.cloned.1.call-update
  10.4 0.2 copy.7
  10.6 0.1 broadcast_in_dim.26
  10.6 0.1 broadcast_in_dim.27
  10.7 2.5 broadcast_in_dim.25
  13.2 0.9 constant_dynamic-update-slice_fusion.7
  14.1 2.2 collective-permute-start
  16.3 0.8 collective-permute-start.1
  17.2 0.4 collective-permute-start.2
  17.6 2.7 collective-permute-start.3
  20.3 0.1 copy.10
  20.4 0.1 broadcast_in_dim.32
  20.4 0.1 reshape.25
  20.5 0.5 broadcast_in_dim.33
  21.1 0.2 constant_dynamic-slice_fusion
  21.4 1.8 copy.12
  23.2 5.4 %collective-permute-done = f32[512,256]{0,1:T(8,128)} collective-permute-done((f32[512,256]{0,1:T(8,128)S(1)}, f32[512,256]{0,1:T(8,128)}, u32[]{:S(2)}, u32[]{:S(2)}) %collective-permute-start) | collective-permute-done | bytes 524320 | tf_op jit(solution)/shard_map/ppermute | solution.py:19
  28.5 1.9 constant_dynamic-update-slice_fusion.6
  30.4 31.7 %collective-permute-done.1 = f32[512,256]{0,1:T(8,128)} collective-permute-done((f32[512,256]{0,1:T(8,128)S(1)}, f32[512,256]{0,1:T(8,128)}, u32[]{:S(2)}, u32[]{:S(2)}) %collective-permute-start.1) | collective-permute-done | bytes 524320 | tf_op jit(solution)/shard_map/ppermute | solution.py:19
  62.1 1.9 constant_dynamic-update-slice_fusion.5
  64.0 1.9 constant_dynamic-update-slice_fusion.4
  65.9 1.9 constant_dynamic-update-slice_fusion.3
  67.8 0.8 constant_dynamic-update-slice_fusion.2
  68.6 0.8 constant_dynamic-update-slice_fusion.1
  69.5 2.5 collective-permute-done.6
  71.9 0.8 constant_dynamic-update-slice_fusion
  72.8 142.6 %all-gather.2.cloned.1.call-done = f32[2048,2048]{0,1:T(8,128)} async-done(((f32[128,2048]{0,1:T(8,128)}), f32[2048,2048]{0,1:T(8,128)}) %all-gather.2.cloned.1.call-update) | async-done | bytes 16777232 | tf_op jit(solution)/shard_map/all_gather | solution.py:41
  215.4 6.4 %fusion.6 = f32[512,256]{1,0:T(8,128)S(1)} fusion(f32[512,2048]{0,1:T(8,128)} %constant_dynamic-update-slice_fusion, f32[2048,2048]{0,1:T(8,128)} %all-gather.2.cloned.1.call-done), kind=kOutput, calls=%fused_computation.6 | convolution fusion | flops 1610612736 | bytes 6815744 | tf_op jit(solution)/shard_map/dot_general | solution.py:25
  221.8 3.2 %collective-permute-start.7 = (f32[512,256]{1,0:T(8,128)S(1)}, f32[512,256]{1,0:T(8,128)S(1)}, u32[]{:S(2)}, u32[]{:S(2)}) collective-permute-start(f32[512,256]{1,0:T(8,128)S(1)} %fusion.6), channel_id=1, source_target_pairs={{0,1},{1,0},{2,3},{3,2},{4,5},{5,4},{6,7},{7,6},{8,9},{9,8},{10,11... | collective-permute-start | bytes 1572872 | tf_op jit(solution)/shard_map/ppermute | solution.py:46
  225.1 10.1 %fusion.2 = f32[512,512]{1,0:T(8,128)S(1)} fusion(f32[512,2048]{0,1:T(8,128)} %constant_dynamic-update-slice_fusion, f32[2048,2048]{0,1:T(8,128)} %all-gather.2.cloned.1.call-done), kind=kOutput, calls=%fused_computation.2 | convolution fusion | flops 3221225472 | bytes 9437184 | tf_op jit(solution)/shard_map/dot_general | solution.py:25
  235.1 3.0 collective-permute-start.9
  238.2 6.3 %fusion.4 = f32[512,256]{1,0:T(8,128)S(1)} fusion(f32[512,2048]{0,1:T(8,128)} %constant_dynamic-update-slice_fusion, f32[2048,2048]{0,1:T(8,128)} %all-gather.2.cloned.1.call-done), kind=kOutput, calls=%fused_computation.4 | convolution fusion | flops 1610612736 | bytes 6815744 | tf_op jit(solution)/shard_map/dot_general | solution.py:25
  244.5 0.0 copy-start
  244.5 3.3 %collective-permute-start.8 = (f32[512,256]{1,0:T(8,128)S(1)}, f32[512,256]{1,0:T(8,128)S(1)}, u32[]{:S(2)}, u32[]{:S(2)}) collective-permute-start(f32[512,256]{1,0:T(8,128)S(1)} %fusion.4), channel_id=1, source_target_pairs={{0,1},{1,0},{2,3},{3,2},{4,5},{5,4},{6,7},{7,6},{8,9},{9,8},{10,11... | collective-permute-start | bytes 1572872 | tf_op jit(solution)/shard_map/ppermute | solution.py:46
  247.8 15.6 %fusion = f32[512,1024]{1,0:T(8,128)S(1)} fusion(f32[512,2048]{0,1:T(8,128)} %constant_dynamic-update-slice_fusion, f32[2048,2048]{0,1:T(8,128)S(1)} %copy-done.1), kind=kOutput, calls=%fused_computation | convolution fusion | flops 6442450944 | bytes 14680064 | tf_op jit(solution)/shard_map/dot_general | solution.py:25
  263.4 13.0 %collective-permute-done.7 = f32[512,256]{1,0:T(8,128)S(1)} collective-permute-done((f32[512,256]{1,0:T(8,128)S(1)}, f32[512,256]{1,0:T(8,128)S(1)}, u32[]{:S(2)}, u32[]{:S(2)}) %collective-permute-start.7) | collective-permute-done | bytes 524320 | tf_op jit(solution)/shard_map/ppermute | solution.py:46
  276.4 34.9 %collective-permute-done.8 = f32[512,256]{1,0:T(8,128)S(1)} collective-permute-done((f32[512,256]{1,0:T(8,128)S(1)}, f32[512,256]{1,0:T(8,128)S(1)}, u32[]{:S(2)}, u32[]{:S(2)}) %collective-permute-start.8) | collective-permute-done | bytes 524320 | tf_op jit(solution)/shard_map/ppermute | solution.py:46
  311.3 1.9 fusion.8
  (18 shorter events, 0.0 us)
Async XLA Ops:
  6.5 208.8 %all-gather.2.cloned.1.call-start = ((), (), s32[]{:S(2)}) async-start(), calls=%async_computation | async-start | bytes 17825792 | tf_op jit(solution)/shard_map/all_gather | solution.py:41
  9.1 1.3 copy-start.2
  9.1 1.5 copy-start.4
  10.3 10.0 %copy-start.3 = (s32[8,32]{1,0:T(8,128)S(1)}, s32[8,32]{1,0:T(8,128)}, u32[]{:S(2)}) copy-start(s32[8,32]{1,0:T(8,128)} %param.9) | copy-start | bytes 3076
  14.1 14.4 %collective-permute-start = (f32[512,256]{0,1:T(8,128)S(1)}, f32[512,256]{0,1:T(8,128)}, u32[]{:S(2)}, u32[]{:S(2)}) collective-permute-start(f32[512,256]{0,1:T(8,128)S(1)} %bitcast.24), channel_id=1, source_target_pairs={{2,0},{4,2},{6,4},{8,6},{10,8},{12,10},{14,12},{0,14},{3,1},{5,3},... | collective-permute-start | bytes 1572872 | tf_op jit(solution)/shard_map/ppermute | solution.py:19
  16.3 45.8 %collective-permute-start.1 = (f32[512,256]{0,1:T(8,128)S(1)}, f32[512,256]{0,1:T(8,128)}, u32[]{:S(2)}, u32[]{:S(2)}) collective-permute-start(f32[512,256]{0,1:T(8,128)S(1)} %bitcast.25), channel_id=1, source_target_pairs={{4,0},{6,2},{8,4},{10,6},{12,8},{14,10},{0,12},{2,14},{5,1},{7,3},... | collective-permute-start | bytes 1572872 | tf_op jit(solution)/shard_map/ppermute | solution.py:19
  17.2 46.8 %collective-permute-start.2 = (f32[512,256]{0,1:T(8,128)S(1)}, f32[512,256]{0,1:T(8,128)}, u32[]{:S(2)}, u32[]{:S(2)}) collective-permute-start(f32[512,256]{0,1:T(8,128)S(1)} %bitcast.26), channel_id=1, source_target_pairs={{6,0},{8,2},{10,4},{12,6},{14,8},{0,10},{2,12},{4,14},{7,1},{9,3},... | collective-permute-start | bytes 1572872 | tf_op jit(solution)/shard_map/ppermute | solution.py:19
  17.6 48.4 %collective-permute-start.3 = (f32[512,256]{0,1:T(8,128)S(1)}, f32[512,256]{0,1:T(8,128)}, u32[]{:S(2)}, u32[]{:S(2)}) collective-permute-start(f32[512,256]{0,1:T(8,128)S(1)} %bitcast.27), channel_id=1, source_target_pairs={{8,0},{10,2},{12,4},{14,6},{0,8},{2,10},{4,12},{6,14},{9,1},{11,3}... | collective-permute-start | bytes 1572872 | tf_op jit(solution)/shard_map/ppermute | solution.py:19
  20.3 47.5 %collective-permute-start.4 = (f32[512,256]{0,1:T(8,128)S(1)}, f32[512,256]{0,1:T(8,128)S(1)}, u32[]{:S(2)}, u32[]{:S(2)}) collective-permute-start(f32[512,256]{0,1:T(8,128)S(1)} %bitcast.28), channel_id=1, source_target_pairs={{10,0},{12,2},{14,4},{0,6},{2,8},{4,10},{6,12},{8,14},{11,1},{13,3... | collective-permute-start | bytes 1572872 | tf_op jit(solution)/shard_map/ppermute | solution.py:19
  28.5 40.1 %collective-permute-start.5 = (f32[512,256]{0,1:T(8,128)S(1)}, f32[512,256]{0,1:T(8,128)S(1)}, u32[]{:S(2)}, u32[]{:S(2)}) collective-permute-start(f32[512,256]{0,1:T(8,128)S(1)} %bitcast.29), channel_id=1, source_target_pairs={{12,0},{14,2},{0,4},{2,6},{4,8},{6,10},{8,12},{10,14},{13,1},{15,3... | collective-permute-start | bytes 1572872 | tf_op jit(solution)/shard_map/ppermute | solution.py:19
  62.1 9.8 %collective-permute-start.6 = (f32[512,256]{0,1:T(8,128)S(1)}, f32[512,256]{0,1:T(8,128)S(1)}, u32[]{:S(2)}, u32[]{:S(2)}) collective-permute-start(f32[512,256]{0,1:T(8,128)S(1)} %bitcast.30), channel_id=1, source_target_pairs={{14,0},{0,2},{2,4},{4,6},{6,8},{8,10},{10,12},{12,14},{15,1},{1,3}... | collective-permute-start | bytes 1572872 | tf_op jit(solution)/shard_map/ppermute | solution.py:19
  215.4 32.4 %copy-start.1 = (f32[2048,2048]{0,1:T(8,128)S(1)}, f32[2048,2048]{0,1:T(8,128)}, u32[]{:S(2)}) copy-start(f32[2048,2048]{0,1:T(8,128)} %all-gather.2.cloned.1.call-done) | copy-start | bytes 50331652
  221.8 54.6 %collective-permute-start.7 = (f32[512,256]{1,0:T(8,128)S(1)}, f32[512,256]{1,0:T(8,128)S(1)}, u32[]{:S(2)}, u32[]{:S(2)}) collective-permute-start(f32[512,256]{1,0:T(8,128)S(1)} %fusion.6), channel_id=1, source_target_pairs={{0,1},{1,0},{2,3},{3,2},{4,5},{5,4},{6,7},{7,6},{8,9},{9,8},{10,11... | collective-permute-start | bytes 1572872 | tf_op jit(solution)/shard_map/ppermute | solution.py:46
  235.1 76.2 %collective-permute-start.9 = (f32[512,512]{1,0:T(8,128)S(1)}, f32[512,512]{1,0:T(8,128)S(1)}, u32[]{:S(2)}, u32[]{:S(2)}) collective-permute-start(f32[512,512]{1,0:T(8,128)S(1)} %fusion.2), channel_id=1, source_target_pairs={{0,1},{1,0},{2,3},{3,2},{4,5},{5,4},{6,7},{7,6},{8,9},{9,8},{10,11... | collective-permute-start | bytes 3145736 | tf_op jit(solution)/shard_map/ppermute | solution.py:46
  244.5 66.8 %copy-start = (f32[512,1024]{1,0:T(8,128)S(1)}, f32[512,1024]{1,0:T(8,128)}, u32[]{:S(2)}) copy-start(f32[512,1024]{1,0:T(8,128)} %copy.12) | copy-start | bytes 6291460
  244.5 66.8 %collective-permute-start.8 = (f32[512,256]{1,0:T(8,128)S(1)}, f32[512,256]{1,0:T(8,128)S(1)}, u32[]{:S(2)}, u32[]{:S(2)}) collective-permute-start(f32[512,256]{1,0:T(8,128)S(1)} %fusion.4), channel_id=1, source_target_pairs={{0,1},{1,0},{2,3},{3,2},{4,5},{5,4},{6,7},{7,6},{8,9},{9,8},{10,11... | collective-permute-start | bytes 1572872 | tf_op jit(solution)/shard_map/ppermute | solution.py:46
Sparse Core Ops, SparseCore 0:
  10.4 204.8 all-gather.1

commit v10 on v7

--- a/solution.py
+++ b/solution.py
@@ -25,6 +25,17 @@
     return jnp.dot(a, b, precision=lax.Precision.HIGH, preferred_element_type=jnp.float32)
 
 
+def split_bf16(x):
+    high = lax.reduce_precision(x, exponent_bits=8, mantissa_bits=7)
+    return high.astype(jnp.bfloat16), (x - high).astype(jnp.bfloat16)
+
+
+def split_dot(a_parts, b):
+    b_parts = split_bf16(b)
+    one = lambda p, q: jnp.dot(p, q, preferred_element_type=jnp.float32)
+    return one(a_parts[0], b_parts[0]) + (one(a_parts[0], b_parts[1]) + one(a_parts[1], b_parts[0]))
+
+
 def shards(density, dens_mask, hamiltonian, ham_mask, filter_mask, n_col):
     layer = lax.axis_index("layer")
     dens_vals = (density * expand(dens_mask))[0]
@@ -41,9 +52,14 @@
     ham_panel = lax.all_gather(jnp.concatenate([send_half, keep_half], axis=1), "row", axis=0, tiled=True)
     dens_row = gather_cols(dens_vals, "col", n_col)
     step = half // 4
+    dens_parts = split_bf16(dens_row)
     received = jnp.concatenate(
         [
-            lax.ppermute(product_dot(dens_row, ham_panel[:, i:i + step]), "layer", [(0, 1), (1, 0)])
+            lax.ppermute(
+                (split_dot(dens_parts, ham_panel[:, i:i + step]) if i == 0 else product_dot(dens_row, ham_panel[:, i:i + step])),
+                "layer",
+                [(0, 1), (1, 0)],
+            )
             for i in range(0, half, step)
         ],
         axis=1,

time: 321 us -> 327 us (1.019)
  matrix products: 40.3 us -> 44.8 us
    dot_general x0 -> x3, matrix products: none -> 12.1 us  [split_dot(): one = lambda p, q: jnp.dot(p, q, preferred_element_type=jnp.float32)]
    dot_general x5 -> x4, matrix products: 40.3 us -> 32.7 us  [product_dot(): jnp.dot(a, b, precision=lax.Precision.HIGH, preferred_element_type=jnp.fl...]
  transfers between devices with their start and end apart: 12 -> 12, of which waited for: 8 -> 8; matrix products, arithmetic and copies ran while one was open for 16% -> 15% of each run, Pallas kernels for 0% -> 0%
where the time goes in v10:
time: 327 us; the launch traced here: 326 us
  waiting for transfers between devices  226 us (69%)
  matrix products  44.8 us (14%)
  starting transfers between devices  18.7 us (6%)
  local copies, waits for them, and re-layouts  17.6 us (5%)
  between operations  13.7 us (4%)
  other arithmetic  4.64 us (1%)
    all_gather x1, waiting for transfers between devices, shards(): lax.all_gather(jnp.concatenate([send_half, keep_half], axis=1), 'row', ax...  143 us
    ppermute x4, waiting for transfers between devices, shards(): lax.ppermute(split_dot(dens_parts, ham_panel[:, i:i + step]) if i == 0 el...  44.2 us
    ppermute x7, waiting for transfers between devices, gather_cols(): lax.ppermute(block, axis_name, [((i + shift) % n, i) for i in range(n)])  39.5 us
    dot_general x4, matrix products, product_dot(): jnp.dot(a, b, precision=lax.Precision.HIGH, preferred_element_type=jnp.fl...  32.7 us
    ppermute x4, starting transfers between devices, shards(): lax.ppermute(split_dot(dens_parts, ham_panel[:, i:i + step]) if i == 0 el...  12.6 us
    dot_general x3, matrix products, split_dot(): one = lambda p, q: jnp.dot(p, q, preferred_element_type=jnp.float32)  12.1 us
    dynamic_update_slice x7, local copies, waits for them, and re-layouts, gather_cols(): lax.dynamic_update_slice_in_dim(full, part, (index + shift) % n * width,...  10 us
  transfers between devices with their start and end apart: 12, of which 8 were waited for; matrix products, arithmetic and copies ran while one was open for 15% of the time, Pallas kernels for 0%

profile of v10, /device:TPU:24, one launch (start us, length us, event | category | flops | bytes accessed | tf_op | source)
XLA Modules:
  0.0 325.8 jit_solution(15391074975420387131)
XLA Ops:
  6.5 0.7 fusion.15
  7.2 0.1 copy.9
  7.3 0.1 broadcast_in_dim.30
  7.4 0.1 reshape.23
  7.5 1.6 copy.8
  9.2 0.1 constant_dynamic-slice_fusion.2
  9.3 1.1 pad_maximum_fusion
  10.4 0.2 copy.7
  10.7 0.1 broadcast_in_dim.27
  10.7 2.5 broadcast_in_dim.25
  13.2 0.9 constant_dynamic-update-slice_fusion.7
  14.1 2.2 collective-permute-start
  16.3 0.8 collective-permute-start.1
  17.2 0.4 collective-permute-start.2
  17.6 2.7 collective-permute-start.3
  20.3 0.1 copy.10
  20.4 0.1 broadcast_in_dim.32
  20.5 0.1 reshape.25
  20.6 0.5 broadcast_in_dim.33
  21.1 0.2 constant_dynamic-slice_fusion
  21.4 1.8 copy.12
  23.2 5.4 %collective-permute-done = f32[512,256]{0,1:T(8,128)} collective-permute-done((f32[512,256]{0,1:T(8,128)S(1)}, f32[512,256]{0,1:T(8,128)}, u32[]{:S(2)}, u32[]{:S(2)}) %collective-permute-start) | collective-permute-done | bytes 524320 | tf_op jit(solution)/shard_map/ppermute | solution.py:19
  28.5 1.9 constant_dynamic-update-slice_fusion.6
  30.4 31.7 %collective-permute-done.1 = f32[512,256]{0,1:T(8,128)} collective-permute-done((f32[512,256]{0,1:T(8,128)S(1)}, f32[512,256]{0,1:T(8,128)}, u32[]{:S(2)}, u32[]{:S(2)}) %collective-permute-start.1) | collective-permute-done | bytes 524320 | tf_op jit(solution)/shard_map/ppermute | solution.py:19
  62.1 1.9 constant_dynamic-update-slice_fusion.5
  64.0 1.9 constant_dynamic-update-slice_fusion.4
  65.9 1.9 constant_dynamic-update-slice_fusion.3
  67.8 0.8 constant_dynamic-update-slice_fusion.2
  68.6 0.8 constant_dynamic-update-slice_fusion.1
  69.5 2.5 collective-permute-done.6
  71.9 0.8 constant_dynamic-update-slice_fusion
  72.8 142.6 %all-gather.2.cloned.1.call-done = f32[2048,2048]{0,1:T(8,128)} async-done(((f32[128,2048]{0,1:T(8,128)}), f32[2048,2048]{0,1:T(8,128)}) %all-gather.2.cloned.1.call-update) | async-done | bytes 16777232 | tf_op jit(solution)/shard_map/all_gather | solution.py:52
  215.4 3.8 %fusion.4 = f32[512,256]{1,0:T(8,128)S(1)} fusion(f32[512,2048]{0,1:T(8,128)} %constant_dynamic-update-slice_fusion, f32[2048,2048]{0,1:T(8,128)} %all-gather.2.cloned.1.call-done), kind=kOutput, calls=%fused_computation.8 | convolution fusion | flops 541065216 | bytes 6815744 | tf_op jit(solution)/shard_map/dot_general | solution.py:35
  219.2 4.2 %convolution_add_fusion = f32[512,256]{1,0:T(8,128)S(1)} fusion(f32[512,256]{1,0:T(8,128)S(1)} %fusion.4, f32[2048,2048]{0,1:T(8,128)} %all-gather.2.cloned.1.call-done, f32[512,2048]{0,1:T(8,128)} %constant_dynamic-update-slice_fusion), kind=kOutput, calls=%fused_computation.17 | convolution fusion | flops 540672000 | bytes 7340032 | tf_op jit(solution)/shard_map/dot_general | solution.py:35
  223.4 4.1 %convolution_add_fusion.1 = f32[512,256]{1,0:T(8,128)S(1)} fusion(f32[512,256]{1,0:T(8,128)S(1)} %convolution_add_fusion, f32[512,2048]{0,1:T(8,128)} %constant_dynamic-update-slice_fusion, f32[2048,2048]{0,1:T(8,128)} %all-gather.2.cloned.1.call-done), kind=kOutput, calls=%fused_computation.18 | convolution fusion | flops 540147712 | bytes 7340032 | tf_op jit(solution)/shard_map/dot_general | solution.py:35
  227.5 3.6 %collective-permute-start.7 = (f32[512,256]{1,0:T(8,128)S(1)}, f32[512,256]{1,0:T(8,128)S(1)}, u32[]{:S(2)}, u32[]{:S(2)}) collective-permute-start(f32[512,256]{1,0:T(8,128)S(1)} %convolution_add_fusion.1), channel_id=1, source_target_pairs={{0,1},{1,0},{2,3},{3,2},{4,5},{5,4},{6,7},{7,6},{8,9},{9,8},{10,11... | collective-permute-start | bytes 1572872 | tf_op jit(solution)/shard_map/ppermute | solution.py:58
  231.1 5.7 %fusion.10 = f32[512,256]{1,0:T(8,128)S(1)} fusion(f32[512,2048]{0,1:T(8,128)} %constant_dynamic-update-slice_fusion, f32[2048,2048]{0,1:T(8,128)S(1)} %copy-done), kind=kOutput, calls=%fused_computation.13 | convolution fusion | flops 1610612736 | bytes 6815744 | tf_op jit(solution)/shard_map/dot_general | solution.py:25
  236.8 2.7 collective-permute-start.8
  239.5 5.7 %fusion.8 = f32[512,256]{1,0:T(8,128)S(1)} fusion(f32[512,2048]{0,1:T(8,128)} %constant_dynamic-update-slice_fusion, f32[2048,2048]{0,1:T(8,128)S(1)} %copy-done), kind=kOutput, calls=%fused_computation.11 | convolution fusion | flops 1610612736 | bytes 6815744 | tf_op jit(solution)/shard_map/dot_general | solution.py:25
  245.2 3.4 %collective-permute-start.9 = (f32[512,256]{1,0:T(8,128)S(1)}, f32[512,256]{1,0:T(8,128)S(1)}, u32[]{:S(2)}, u32[]{:S(2)}) collective-permute-start(f32[512,256]{1,0:T(8,128)S(1)} %fusion.8), channel_id=1, source_target_pairs={{0,1},{1,0},{2,3},{3,2},{4,5},{5,4},{6,7},{7,6},{8,9},{9,8},{10,11... | collective-permute-start | bytes 1572872 | tf_op jit(solution)/shard_map/ppermute | solution.py:58
  248.6 5.7 %fusion.6 = f32[512,256]{1,0:T(8,128)S(1)} fusion(f32[512,2048]{0,1:T(8,128)} %constant_dynamic-update-slice_fusion, f32[2048,2048]{0,1:T(8,128)S(1)} %copy-done), kind=kOutput, calls=%fused_computation.9 | convolution fusion | flops 1610612736 | bytes 6815744 | tf_op jit(solution)/shard_map/dot_general | solution.py:25
  254.3 2.9 collective-permute-start.10
  257.2 15.6 %fusion = f32[512,1024]{1,0:T(8,128)S(1)} fusion(f32[512,2048]{0,1:T(8,128)} %constant_dynamic-update-slice_fusion, f32[2048,2048]{0,1:T(8,128)S(1)} %copy-done), kind=kOutput, calls=%fused_computation | convolution fusion | flops 6442450944 | bytes 14680064 | tf_op jit(solution)/shard_map/dot_general | solution.py:25
  272.8 3.3 %collective-permute-done.7 = f32[512,256]{1,0:T(8,128)S(1)} collective-permute-done((f32[512,256]{1,0:T(8,128)S(1)}, f32[512,256]{1,0:T(8,128)S(1)}, u32[]{:S(2)}, u32[]{:S(2)}) %collective-permute-start.7) | collective-permute-done | bytes 524320 | tf_op jit(solution)/shard_map/ppermute | solution.py:58
  276.2 24.0 %collective-permute-done.8 = f32[512,256]{1,0:T(8,128)S(1)} collective-permute-done((f32[512,256]{1,0:T(8,128)S(1)}, f32[512,256]{1,0:T(8,128)S(1)}, u32[]{:S(2)}, u32[]{:S(2)}) %collective-permute-start.8) | collective-permute-done | bytes 524320 | tf_op jit(solution)/shard_map/ppermute | solution.py:58
  300.2 11.2 %collective-permute-done.9 = f32[512,256]{1,0:T(8,128)S(1)} collective-permute-done((f32[512,256]{1,0:T(8,128)S(1)}, f32[512,256]{1,0:T(8,128)S(1)}, u32[]{:S(2)}, u32[]{:S(2)}) %collective-permute-start.9) | collective-permute-done | bytes 524320 | tf_op jit(solution)/shard_map/ppermute | solution.py:58
  311.4 5.6 %collective-permute-done.10 = f32[512,256]{1,0:T(8,128)S(1)} collective-permute-done((f32[512,256]{1,0:T(8,128)S(1)}, f32[512,256]{1,0:T(8,128)S(1)}, u32[]{:S(2)}, u32[]{:S(2)}) %collective-permute-start.10) | collective-permute-done | bytes 524320 | tf_op jit(solution)/shard_map/ppermute | solution.py:58
  317.1 1.9 fusion.12
  (23 shorter events, 0.2 us)
Async XLA Ops:
  6.5 208.8 %all-gather.2.cloned.1.call-start = ((), (), s32[]{:S(2)}) async-start(), calls=%async_computation | async-start | bytes 17825792 | tf_op jit(solution)/shard_map/all_gather | solution.py:52
  9.1 1.3 copy-start.2
  9.1 1.5 copy-start.4
  10.3 10.0 %copy-start.3 = (s32[8,32]{1,0:T(8,128)S(1)}, s32[8,32]{1,0:T(8,128)}, u32[]{:S(2)}) copy-start(s32[8,32]{1,0:T(8,128)} %param.9) | copy-start | bytes 3076
  14.1 14.4 %collective-permute-start = (f32[512,256]{0,1:T(8,128)S(1)}, f32[512,256]{0,1:T(8,128)}, u32[]{:S(2)}, u32[]{:S(2)}) collective-permute-start(f32[512,256]{0,1:T(8,128)S(1)} %bitcast.24), channel_id=1, source_target_pairs={{2,0},{4,2},{6,4},{8,6},{10,8},{12,10},{14,12},{0,14},{3,1},{5,3},... | collective-permute-start | bytes 1572872 | tf_op jit(solution)/shard_map/ppermute | solution.py:19
  16.3 45.8 %collective-permute-start.1 = (f32[512,256]{0,1:T(8,128)S(1)}, f32[512,256]{0,1:T(8,128)}, u32[]{:S(2)}, u32[]{:S(2)}) collective-permute-start(f32[512,256]{0,1:T(8,128)S(1)} %bitcast.25), channel_id=1, source_target_pairs={{4,0},{6,2},{8,4},{10,6},{12,8},{14,10},{0,12},{2,14},{5,1},{7,3},... | collective-permute-start | bytes 1572872 | tf_op jit(solution)/shard_map/ppermute | solution.py:19
  17.2 46.8 %collective-permute-start.2 = (f32[512,256]{0,1:T(8,128)S(1)}, f32[512,256]{0,1:T(8,128)}, u32[]{:S(2)}, u32[]{:S(2)}) collective-permute-start(f32[512,256]{0,1:T(8,128)S(1)} %bitcast.26), channel_id=1, source_target_pairs={{6,0},{8,2},{10,4},{12,6},{14,8},{0,10},{2,12},{4,14},{7,1},{9,3},... | collective-permute-start | bytes 1572872 | tf_op jit(solution)/shard_map/ppermute | solution.py:19
  17.6 48.3 %collective-permute-start.3 = (f32[512,256]{0,1:T(8,128)S(1)}, f32[512,256]{0,1:T(8,128)}, u32[]{:S(2)}, u32[]{:S(2)}) collective-permute-start(f32[512,256]{0,1:T(8,128)S(1)} %bitcast.27), channel_id=1, source_target_pairs={{8,0},{10,2},{12,4},{14,6},{0,8},{2,10},{4,12},{6,14},{9,1},{11,3}... | collective-permute-start | bytes 1572872 | tf_op jit(solution)/shard_map/ppermute | solution.py:19
  20.3 47.5 %collective-permute-start.4 = (f32[512,256]{0,1:T(8,128)S(1)}, f32[512,256]{0,1:T(8,128)S(1)}, u32[]{:S(2)}, u32[]{:S(2)}) collective-permute-start(f32[512,256]{0,1:T(8,128)S(1)} %bitcast.28), channel_id=1, source_target_pairs={{10,0},{12,2},{14,4},{0,6},{2,8},{4,10},{6,12},{8,14},{11,1},{13,3... | collective-permute-start | bytes 1572872 | tf_op jit(solution)/shard_map/ppermute | solution.py:19
  28.5 40.1 %collective-permute-start.5 = (f32[512,256]{0,1:T(8,128)S(1)}, f32[512,256]{0,1:T(8,128)S(1)}, u32[]{:S(2)}, u32[]{:S(2)}) collective-permute-start(f32[512,256]{0,1:T(8,128)S(1)} %bitcast.29), channel_id=1, source_target_pairs={{12,0},{14,2},{0,4},{2,6},{4,8},{6,10},{8,12},{10,14},{13,1},{15,3... | collective-permute-start | bytes 1572872 | tf_op jit(solution)/shard_map/ppermute | solution.py:19
  62.1 9.8 %collective-permute-start.6 = (f32[512,256]{0,1:T(8,128)S(1)}, f32[512,256]{0,1:T(8,128)S(1)}, u32[]{:S(2)}, u32[]{:S(2)}) collective-permute-start(f32[512,256]{0,1:T(8,128)S(1)} %bitcast.30), channel_id=1, source_target_pairs={{14,0},{0,2},{2,4},{4,6},{6,8},{8,10},{10,12},{12,14},{15,1},{1,3}... | collective-permute-start | bytes 1572872 | tf_op jit(solution)/shard_map/ppermute | solution.py:19
  215.4 15.7 %copy-start = (f32[2048,2048]{0,1:T(8,128)S(1)}, f32[2048,2048]{0,1:T(8,128)}, u32[]{:S(2)}) copy-start(f32[2048,2048]{0,1:T(8,128)} %all-gather.2.cloned.1.call-done) | copy-start | bytes 50331652
  227.5 48.7 %collective-permute-start.7 = (f32[512,256]{1,0:T(8,128)S(1)}, f32[512,256]{1,0:T(8,128)S(1)}, u32[]{:S(2)}, u32[]{:S(2)}) collective-permute-start(f32[512,256]{1,0:T(8,128)S(1)} %convolution_add_fusion.1), channel_id=1, source_target_pairs={{0,1},{1,0},{2,3},{3,2},{4,5},{5,4},{6,7},{7,6},{8,9},{9,8},{10,11... | collective-permute-start | bytes 1572872 | tf_op jit(solution)/shard_map/ppermute | solution.py:58
  236.8 63.4 %collective-permute-start.8 = (f32[512,256]{1,0:T(8,128)S(1)}, f32[512,256]{1,0:T(8,128)S(1)}, u32[]{:S(2)}, u32[]{:S(2)}) collective-permute-start(f32[512,256]{1,0:T(8,128)S(1)} %fusion.10), channel_id=1, source_target_pairs={{0,1},{1,0},{2,3},{3,2},{4,5},{5,4},{6,7},{7,6},{8,9},{9,8},{10,11... | collective-permute-start | bytes 1572872 | tf_op jit(solution)/shard_map/ppermute | solution.py:58
  245.2 66.3 %collective-permute-start.9 = (f32[512,256]{1,0:T(8,128)S(1)}, f32[512,256]{1,0:T(8,128)S(1)}, u32[]{:S(2)}, u32[]{:S(2)}) collective-permute-start(f32[512,256]{1,0:T(8,128)S(1)} %fusion.8), channel_id=1, source_target_pairs={{0,1},{1,0},{2,3},{3,2},{4,5},{5,4},{6,7},{7,6},{8,9},{9,8},{10,11... | collective-permute-start | bytes 1572872 | tf_op jit(solution)/shard_map/ppermute | solution.py:58
  254.3 62.8 %copy-start.1 = (f32[512,1024]{1,0:T(8,128)S(1)}, f32[512,1024]{1,0:T(8,128)}, u32[]{:S(2)}) copy-start(f32[512,1024]{1,0:T(8,128)} %copy.12) | copy-start | bytes 6291460
  254.3 62.8 %collective-permute-start.10 = (f32[512,256]{1,0:T(8,128)S(1)}, f32[512,256]{1,0:T(8,128)S(1)}, u32[]{:S(2)}, u32[]{:S(2)}) collective-permute-start(f32[512,256]{1,0:T(8,128)S(1)} %fusion.6), channel_id=1, source_target_pairs={{0,1},{1,0},{2,3},{3,2},{4,5},{5,4},{6,7},{7,6},{8,9},{9,8},{10,11... | collective-permute-start | bytes 1572872 | tf_op jit(solution)/shard_map/ppermute | solution.py:58
Sparse Core Ops, SparseCore 0:
  10.5 204.8 all-gather.1
